TPU v7x, 256 devices: a whole 4x4x8 slice. The times are simulated.
256 devices in a mesh: seq: 64 (over y, z, core), txt: 4 (over x).
Axes of the slice: x: 4, y: 4, z: 8, core: 2. Of those that a mesh axis runs over, the one named last changes fastest.
Arguments:
- self_q: bfloat16 [24576, 1024], P('seq', 'txt'), may hold values from -8 to 8
- self_k: bfloat16 [24576, 1024], P('seq', 'txt'), may hold values from -8 to 8
- self_v: bfloat16 [24576, 1024], P('seq', 'txt'), may hold values from -6 to 6
- cross_q: bfloat16 [24576, 1024], P('seq', 'txt'), may hold values from -8 to 8
- text_k: bfloat16 [4096, 1024], P('txt'), may hold values from -8 to 8
- text_v: bfloat16 [4096, 1024], P('txt'), may hold values from -6 to 6
- lags: int32 [192], P('seq'), may hold values from 1 to 32, as said below
Outputs:
- self_out: bfloat16 [24576, 1024], P('seq', 'txt')
- cross_out: bfloat16 [24576, 1024], P('seq', 'txt')
Inputs may be any that keep to these rules, and one draw needn't show every extreme that they name: lags never fall from one span to the next; the last span sees all 32 blocks.
All inputs are finite; a program needn't handle non-finite values.
Results may differ from a plain program's by a relative error of at most 0.014.
Values may be sent and summed in bfloat16 or wider, within the bound.
No kernel may reach another device: no remote copies, remote signals or barrier semaphores. Data moves between devices by JAX's collectives and lax.ppermute only.
A program may use at most 128 MiB of HBM per device.

v0:
```python
import math

import jax
import jax.numpy as jnp
from jax import lax
from jax.sharding import PartitionSpec as P

HSIZE = 128
SPAN = 128
TBLK = 128


NEG_FILL = -1e30


def scale_columns(weighted, scale):
    rows = weighted.shape[0]
    heads = scale.shape[0]
    shaped = weighted.reshape(rows, heads, weighted.shape[1] // heads)
    return (shaped * jnp.transpose(scale)[:, :, None]).reshape(rows, weighted.shape[1])


def softmax_update(state, query, keys, values, visible, factor):
    running, totals, weighted = state
    heads = running.shape[0]
    peaks = []
    sums = []
    columns = []
    for head in range(heads):
        low = head * HSIZE
        high = low + HSIZE
        scores = (
            lax.dot_general(
                query[:, low:high],
                keys[:, low:high],
                (((1,), (1,)), ((), ())),
                preferred_element_type=jnp.float32,
            )
            * factor
        )
        scores = jnp.where(visible, scores, NEG_FILL)
        peak = jnp.maximum(running[head], jnp.max(scores, axis=1))
        probs = jnp.where(visible, jnp.exp(scores - peak[:, None]), 0.0)
        shrink = jnp.exp(running[head] - peak)
        sums.append(totals[head] * shrink + jnp.sum(probs, axis=1))
        mixed = jnp.dot(
            probs.astype(jnp.bfloat16), values[:, low:high], preferred_element_type=jnp.float32
        )
        columns.append(weighted[:, low:high] * shrink[:, None] + mixed)
        peaks.append(peak)
    return (jnp.stack(peaks), jnp.stack(sums), jnp.concatenate(columns, axis=1))


def empty_state(heads, rows, width):
    return (
        jnp.full((heads, rows), NEG_FILL, jnp.float32),
        jnp.zeros((heads, rows), jnp.float32),
        jnp.zeros((rows, heads * width), jnp.float32),
    )


def finish(state):
    return scale_columns(state[2], 1.0 / state[1]).astype(jnp.bfloat16)


def per_device(self_q, self_k, self_v, cross_q, text_k, text_v, lags):
    rows = self_q.shape[0]
    half = rows // 2
    local_heads = self_q.shape[1] // HSIZE
    factor = 1.0 / math.sqrt(HSIZE)
    place = lax.axis_index("seq")
    offsets = jnp.arange(half, dtype=jnp.int32)
    lower = self_q[:half]
    upper = self_q[half:]
    upper_pos = place * rows + half + offsets
    positions = [place * rows + offsets, upper_pos]
    groups = [lower, upper]

    def visit(states, key_block, value_block, first, length):
        key_pos = first + jnp.arange(length, dtype=jnp.int32)
        updated = []
        for group in range(2):
            visible = key_pos[None, :] <= positions[group][:, None]
            query = groups[group]
            updated.append(
                lax.cond(
                    first <= positions[group][half - 1],
                    lambda state: softmax_update(
                        state, query, key_block, value_block, visible, factor
                    ),
                    lambda state: state,
                    states[group],
                )
            )
        return tuple(updated)

    initial = (empty_state(local_heads, half, HSIZE), empty_state(local_heads, half, HSIZE))
    carry = initial
    keys = lax.all_gather(self_k, "seq", axis=0, tiled=True)
    values = lax.all_gather(self_v, "seq", axis=0, tiled=True)
    length = keys.shape[0]
    block = 512
    width = keys.shape[1]
    key_blocks = keys.reshape(length // block, block, width)
    value_blocks = values.reshape(length // block, block, width)

    def one_block(states, inputs):
        key_block, value_block, number = inputs
        return (visit(states, key_block, value_block, number * block, block), None)

    carry, _ = lax.scan(
        one_block, carry, (key_blocks, value_blocks, jnp.arange(length // block, dtype=jnp.int32))
    )
    states = carry
    lower_out = finish(states[0])
    upper_out = finish(states[1])
    self_out = jnp.concatenate([lower_out, upper_out], axis=0)
    limits = jnp.repeat(lags * TBLK, SPAN)
    whole_keys, whole_values = (
        lax.all_to_all(text_k, "txt", split_axis=1, concat_axis=0, tiled=True),
        lax.all_to_all(text_v, "txt", split_axis=1, concat_axis=0, tiled=True),
    )
    text_rows = whole_keys.shape[0]
    visible = jnp.arange(text_rows, dtype=jnp.int32)[None, :] < limits[:, None]
    cross_state = softmax_update(
        empty_state(local_heads, rows, HSIZE), cross_q, whole_keys, whole_values, visible, factor
    )
    cross_out = finish(cross_state)
    return (self_out, cross_out)


def solution(mesh):
    return jax.shard_map(
        per_device,
        mesh=mesh,
        in_specs=(
            P("seq", "txt"),
            P("seq", "txt"),
            P("seq", "txt"),
            P("seq", "txt"),
            P("txt", None),
            P("txt", None),
            P("seq"),
        ),
        out_specs=(P("seq", "txt"), P("seq", "txt")),
        check_vma=False,
    )
```

profile of v0, /device:TPU:249, one launch (start us, length us, event | category | flops | bytes accessed | tf_op | source)
XLA Modules:
  0.0 571.9 jit_solution(3053998208419744763)
XLA Ops:
  8.6 3.9 copy.17
  12.6 4.1 all-to-all-start
  16.7 3.9 copy.19
  20.7 21.6 %all-to-all-done = bf16[1024,4,256]{0,2,1:T(8,128)(2,1)S(1)} async-done(((bf16[1024,4,256]{0,2,1:T(8,128)(2,1)}), bf16[1024,4,256]{0,2,1:T(8,128)(2,1)S(1)}, u32[]{:S(2)}, u32[]{:S(2)}) %all-to-all-start) | async-done | bytes 2097184 | tf_op jit(solution)/shard_map/all_to_all | solution.py:120
  42.2 4.6 all-to-all-start.1
  46.9 2.6 copy.18
  49.5 21.9 %all-to-all-done.1 = bf16[1024,4,256]{0,2,1:T(8,128)(2,1)} async-done(((bf16[1024,4,256]{0,2,1:T(8,128)(2,1)}), bf16[1024,4,256]{0,2,1:T(8,128)(2,1)}, u32[]{:S(2)}, u32[]{:S(2)}) %all-to-all-start.1) | async-done | bytes 2097184 | tf_op jit(solution)/shard_map/all_to_all | solution.py:121
  71.5 2.9 copy.20
  74.4 2.8 fusion.83
  78.6 3.3 fusion.48
  81.9 1.6 fusion.59
  83.6 1.6 fusion.56
  86.1 11.4 %all-gather.3.cloned.1.call-done = bf16[24576,256]{1,0:T(8,128)(2,1)} async-done(((bf16[384,256]{1,0:T(8,128)(2,1)}), bf16[24576,256]{1,0:T(8,128)(2,1)}) %all-gather.3.cloned.1.call-update) | async-done | bytes 12582928 | tf_op jit(solution)/shard_map/all_gather | solution.py:99
  97.5 89.2 %all-gather.5.cloned.1.call-done = bf16[24576,256]{1,0:T(8,128)(2,1)} async-done(((bf16[384,256]{1,0:T(8,128)(2,1)}), bf16[24576,256]{1,0:T(8,128)(2,1)}) %all-gather.5.cloned.1.call-update) | async-done | bytes 12582928 | tf_op jit(solution)/shard_map/all_gather | solution.py:100
  186.7 376.7 %while.20 = (s32[]{:T(128)}, f32[2,192]{1,0:T(2,128)S(1)}, f32[2,192]{1,0:T(2,128)S(1)}, f32[192,256]{1,0:T(8,128)S(1)}, f32[2,192]{1,0:T(2,128)S(1)}, /*index=5...) while((s32[]{:T(128)}, f32[2,192]{1,0:T(2,128)S(1)}, ...), condition=%wide.region_13.14_spmd, body=%wide.region_0.13_spmd.sunk | while | flops 206148608 | bytes 8684505 | solution.py:111
  190.2 1.6 conditional.4
  198.0 1.6 conditional.4
  205.9 1.6 conditional.4
  213.7 1.6 conditional.4
  221.6 1.6 conditional.4
  229.4 1.6 conditional.4
  237.3 1.6 conditional.4
  245.1 1.6 conditional.4
  253.0 1.6 conditional.4
  284.4 1.6 conditional.4
  292.2 1.6 conditional.4
  300.1 1.6 conditional.4
  307.9 1.6 conditional.4
  315.8 1.6 conditional.4
  323.6 1.6 conditional.4
  331.5 1.6 conditional.4
  339.3 1.6 conditional.4
  347.2 1.6 conditional.4
  355.0 1.6 conditional.4
  362.9 1.6 conditional.4
  370.7 1.6 conditional.4
  378.6 1.6 conditional.4
  386.4 1.6 conditional.4
  394.3 1.6 conditional.4
  402.1 1.6 conditional.4
  433.5 1.6 conditional.4
  441.3 1.6 conditional.4
  449.2 1.6 conditional.4
  457.0 1.6 conditional.4
  464.9 1.6 conditional.4
  472.7 1.6 conditional.4
  480.6 1.6 conditional.4
  488.4 1.6 conditional.4
  (1400 shorter events, 391.4 us)
Async XLA Ops:
  7.2 90.3 %all-gather.3.cloned.1.call-start = ((), (), s32[]{:S(2)}) async-start(), calls=%async_computation.2 | async-start | bytes 12779520 | tf_op jit(solution)/shard_map/all_gather | solution.py:99
  7.9 178.8 %all-gather.5.cloned.1.call-start = ((), (), s32[]{:S(2)}) async-start(), calls=%async_computation.3 | async-start | bytes 12779520 | tf_op jit(solution)/shard_map/all_gather | solution.py:100
  12.6 34.2 %copy-start.3 = (s32[3]{0:T(128)S(1)}, s32[3]{0:T(128)}, u32[]{:S(2)}) copy-start(s32[3]{0:T(128)} %param.19) | copy-start | bytes 40
  12.6 34.3 %copy-start.1 = (bf16[384,256]{1,0:T(8,128)(2,1)S(1)}, bf16[384,256]{1,0:T(8,128)(2,1)}, u32[]{:S(2)}) copy-start(bf16[384,256]{1,0:T(8,128)(2,1)} %param.13) | copy-start | bytes 589828
  12.6 29.6 %all-to-all-start = ((bf16[1024,4,256]{0,2,1:T(8,128)(2,1)}), bf16[1024,4,256]{0,2,1:T(8,128)(2,1)S(1)}, u32[]{:S(2)}, u32[]{:S(2)}) async-start(bf16[1024,4,256]{0,2,1:T(8,128)(2,1)} %bitcast.57), calls=%async_computation | async-start | bytes 4194304 | tf_op jit(solution)/shard_map/all_to_all | solution.py:120
  42.2 32.2 %copy-start.2 = (bf16[384,256]{1,0:T(8,128)(2,1)S(1)}, bf16[384,256]{1,0:T(8,128)(2,1)}, u32[]{:S(2)}) copy-start(bf16[384,256]{1,0:T(8,128)(2,1)} %param.16) | copy-start | bytes 589828
  42.2 29.3 %all-to-all-start.1 = ((bf16[1024,4,256]{0,2,1:T(8,128)(2,1)}), bf16[1024,4,256]{0,2,1:T(8,128)(2,1)}, u32[]{:S(2)}, u32[]{:S(2)}) async-start(bf16[1024,4,256]{0,2,1:T(8,128)(2,1)} %bitcast.56), calls=%async_computation.1 | async-start | bytes 4194304 | tf_op jit(solution)/shard_map/all_to_all | solution.py:121
  74.4 2.8 copy-start
Sparse Core Ops, SparseCore 0:
  10.7 86.6 all-gather.2
  100.2 86.4 all-gather.4
where the time goes:
time: 574 us; the launch traced here: 572 us
  local copies, waits for them, and re-layouts  149 us (26%)
  waiting for transfers between devices  145 us (25%)
  matrix products  118 us (21%)
  loops' own time  93.5 us (16%)
  other arithmetic  42.7 us (7%)
  between operations  14.3 us (2%)
  starting transfers between devices  8.81 us (2%)
    all_gather x1, waiting for transfers between devices, per_device(): values = lax.all_gather(self_v, 'seq', axis=0, tiled=True)  89.2 us
    another operation x1, loops' own time, per_device(): lax.scan(one_block, carry, (key_blocks, value_blocks, jnp.arange(length /...  86.1 us
    dot_general x194, matrix products, softmax_update(): lax.dot_general(query[:, low:high], keys[:, low:high], (((1,), (1,)), (()...  63.3 us
    dot_general x194, matrix products, softmax_update(): jnp.dot(probs.astype(jnp.bfloat16), values[:, low:high], preferred_elemen...  54.7 us
    slice x96, local copies, waits for them, and re-layouts, visit(): positions[group][half - 1]  53 us
    squeeze x48, local copies, waits for them, and re-layouts, per_device(): lax.scan(one_block, carry, (key_blocks, value_blocks, jnp.arange(length /...  51.4 us
    reduce_sum x97, other arithmetic, softmax_update(): sums.append(totals[head] * shrink + jnp.sum(probs, axis=1))  36 us
    dynamic_slice x48, local copies, waits for them, and re-layouts, per_device(): lax.scan(one_block, carry, (key_blocks, value_blocks, jnp.arange(length /...  29.3 us
  transfers between devices with their start and end apart: 4, of which 4 were waited for; matrix products, arithmetic and copies ran while one was open for 4% of the time, Pallas kernels for 0%

commit v1 on v0

v1 whole, which is shorter than its diff:
```python
import functools
import math

import jax
import jax.numpy as jnp
import numpy as np
from jax import lax
from jax.experimental import pallas as pl
from jax.experimental.pallas import tpu as pltpu
from jax.sharding import Mesh
from jax.sharding import PartitionSpec as P

HSIZE = 128
SPAN = 128
TBLK = 128

NEG_FILL = -1e30
FACTOR = 1.0 / math.sqrt(HSIZE)


def online_step(q, k, v, mask, m_ref, l_ref, acc_ref):
    scores = (
        lax.dot_general(q, k, (((1,), (1,)), ((), ())), preferred_element_type=jnp.float32)
        * FACTOR
    )
    if mask is not None:
        scores = jnp.where(mask, scores, NEG_FILL)
    m_prev = m_ref[...]
    m_next = jnp.maximum(m_prev, jnp.max(scores, axis=1, keepdims=True))
    probs = jnp.exp(scores - m_next[:, 0:1])
    if mask is not None:
        probs = jnp.where(mask, probs, 0.0)
    alpha = jnp.exp(m_prev - m_next)
    l_ref[...] = alpha * l_ref[...] + jnp.sum(probs, axis=1, keepdims=True)
    mixed = jnp.dot(probs.astype(jnp.bfloat16), v, preferred_element_type=jnp.float32)
    acc_ref[...] = acc_ref[...] * alpha + mixed
    m_ref[...] = m_next


def self_kernel(info_ref, q_ref, k_ref, v_ref, o_ref, lse_ref, m_ref, l_ref, acc_ref):
    t = pl.program_id(0)
    kb = pl.program_id(1)
    nkb = pl.num_programs(1)
    qblk = info_ref[t]
    core = info_ref[2]
    last = (qblk - core + 2) // 2 - 1

    @pl.when(kb == 0)
    def _():
        m_ref[...] = jnp.full(m_ref.shape, NEG_FILL, jnp.float32)
        l_ref[...] = jnp.zeros(l_ref.shape, jnp.float32)
        acc_ref[...] = jnp.zeros(acc_ref.shape, jnp.float32)

    diag = 2 * kb + core == qblk

    @pl.when(jnp.logical_and(kb <= last, jnp.logical_not(diag)))
    def _():
        online_step(q_ref[...], k_ref[...], v_ref[...], None, m_ref, l_ref, acc_ref)

    @pl.when(jnp.logical_and(kb <= last, diag))
    def _():
        rows = q_ref.shape[0]
        cols = k_ref.shape[0]
        r = lax.broadcasted_iota(jnp.int32, (rows, cols), 0)
        j = lax.broadcasted_iota(jnp.int32, (rows, cols), 1)
        online_step(q_ref[...], k_ref[...], v_ref[...], j <= r, m_ref, l_ref, acc_ref)

    @pl.when(kb == nkb - 1)
    def _():
        l = l_ref[...]
        seen = l > 0.0
        o_ref[...] = acc_ref[...] / jnp.where(seen, l, 1.0)
        lse_ref[...] = jnp.where(seen, m_ref[...] + jnp.log(jnp.where(seen, l, 1.0)), NEG_FILL)


def self_partial(info, q2, keys, values):
    block = q2.shape[0] // 2
    nkb = keys.shape[0] // block

    def kv_map(t, kb, info_ref):
        last = (info_ref[t] - info_ref[2] + 2) // 2 - 1
        return (jnp.maximum(jnp.minimum(kb, last), 0), 0)

    grid_spec = pltpu.PrefetchScalarGridSpec(
        num_scalar_prefetch=1,
        grid=(2, nkb),
        in_specs=[
            pl.BlockSpec((block, HSIZE), lambda t, kb, info_ref: (t, 0)),
            pl.BlockSpec((block, HSIZE), kv_map),
            pl.BlockSpec((block, HSIZE), kv_map),
        ],
        out_specs=[
            pl.BlockSpec((block, HSIZE), lambda t, kb, info_ref: (t, 0)),
            pl.BlockSpec((block, HSIZE), lambda t, kb, info_ref: (t, 0)),
        ],
        scratch_shapes=[
            pltpu.VMEM((block, HSIZE), jnp.float32),
            pltpu.VMEM((block, HSIZE), jnp.float32),
            pltpu.VMEM((block, HSIZE), jnp.float32),
        ],
    )
    rows = q2.shape[0]
    flops = 2 * 2 * rows * keys.shape[0] * HSIZE // 2
    return pl.pallas_call(
        self_kernel,
        grid_spec=grid_spec,
        out_shape=[
            jax.ShapeDtypeStruct((rows, HSIZE), jnp.float32),
            jax.ShapeDtypeStruct((rows, HSIZE), jnp.float32),
        ],
        compiler_params=pltpu.CompilerParams(dimension_semantics=("arbitrary", "arbitrary")),
        cost_estimate=pl.CostEstimate(
            flops=flops,
            transcendentals=rows * keys.shape[0] // 2,
            bytes_accessed=keys.size * 2 + values.size * 2 + rows * HSIZE * 10,
        ),
    )(info, q2, keys, values)


def cross_kernel(info_ref, q_ref, k_ref, v_ref, o_ref, m_ref, l_ref, acc_ref):
    kb = pl.program_id(1)
    nkb = pl.num_programs(1)
    tk = k_ref.shape[0]
    rows = q_ref.shape[0]
    last = info_ref[3]

    @pl.when(kb == 0)
    def _():
        m_ref[...] = jnp.full(m_ref.shape, NEG_FILL, jnp.float32)
        l_ref[...] = jnp.zeros(l_ref.shape, jnp.float32)
        acc_ref[...] = jnp.zeros(acc_ref.shape, jnp.float32)

    @pl.when(kb <= last)
    def _():
        r = lax.broadcasted_iota(jnp.int32, (rows, tk), 0)
        j = lax.broadcasted_iota(jnp.int32, (rows, tk), 1) + kb * tk
        span = r // SPAN
        limit = jnp.where(span == 0, info_ref[0], jnp.where(span == 1, info_ref[1], info_ref[2]))
        online_step(q_ref[...], k_ref[...], v_ref[...], j < limit * TBLK, m_ref, l_ref, acc_ref)

    @pl.when(kb == nkb - 1)
    def _():
        o_ref[...] = (acc_ref[...] / l_ref[...]).astype(o_ref.dtype)


def cross_attention(info, query, keys, values):
    rows = query.shape[0]
    heads = query.shape[1] // HSIZE
    tk = 512
    nkb = keys.shape[0] // tk

    def kv_map(h, kb, info_ref):
        return (jnp.minimum(kb, info_ref[3]), h)

    grid_spec = pltpu.PrefetchScalarGridSpec(
        num_scalar_prefetch=1,
        grid=(heads, nkb),
        in_specs=[
            pl.BlockSpec((rows, HSIZE), lambda h, kb, info_ref: (0, h)),
            pl.BlockSpec((tk, HSIZE), kv_map),
            pl.BlockSpec((tk, HSIZE), kv_map),
        ],
        out_specs=pl.BlockSpec((rows, HSIZE), lambda h, kb, info_ref: (0, h)),
        scratch_shapes=[
            pltpu.VMEM((rows, HSIZE), jnp.float32),
            pltpu.VMEM((rows, HSIZE), jnp.float32),
            pltpu.VMEM((rows, HSIZE), jnp.float32),
        ],
    )
    return pl.pallas_call(
        cross_kernel,
        grid_spec=grid_spec,
        out_shape=jax.ShapeDtypeStruct(query.shape, jnp.bfloat16),
        compiler_params=pltpu.CompilerParams(dimension_semantics=("arbitrary", "arbitrary")),
        cost_estimate=pl.CostEstimate(
            flops=4 * rows * keys.shape[0] * query.shape[1],
            transcendentals=rows * keys.shape[0] * heads,
            bytes_accessed=keys.size * 2 + values.size * 2 + query.size * 4,
        ),
    )(info, query, keys, values)


def merge(o_a, lse_a, o_b, lse_b):
    top = jnp.maximum(lse_a, lse_b)
    w_a = jnp.exp(lse_a - top)
    w_b = jnp.exp(lse_b - top)
    return (o_a * w_a + o_b * w_b) / (w_a + w_b)


def per_device(self_q, self_k, self_v, cross_q, text_k, text_v, lags):
    rows = self_q.shape[0]
    heads = self_q.shape[1] // HSIZE
    chip = lax.axis_index("chip")
    core = lax.axis_index("core")
    swap = [(0, 1), (1, 0)]
    info = jnp.stack([2 * chip + core, 2 * chip + 1 - core, core]).astype(jnp.int32)

    whole_keys = lax.all_to_all(text_k, "txt", split_axis=1, concat_axis=0, tiled=True)
    whole_values = lax.all_to_all(text_v, "txt", split_axis=1, concat_axis=0, tiled=True)

    outs = []
    for h in range(heads):
        cols = slice(h * HSIZE, (h + 1) * HSIZE)
        q_h = self_q[:, cols]
        keys = lax.all_gather(self_k[:, cols], "chip", axis=0, tiled=True)
        values = lax.all_gather(self_v[:, cols], "chip", axis=0, tiled=True)
        q2 = jnp.concatenate([q_h, lax.ppermute(q_h, "core", swap)], axis=0)
        o_part, lse_part = self_partial(info, q2, keys, values)
        o_back = lax.ppermute(o_part[rows:], "core", swap)
        lse_back = lax.ppermute(lse_part[rows:], "core", swap)
        outs.append(merge(o_part[:rows], lse_part[:rows], o_back, lse_back).astype(jnp.bfloat16))
    self_out = jnp.concatenate(outs, axis=1)

    top = jnp.max(lags)
    cross_info = jnp.concatenate(
        [lags.astype(jnp.int32), ((top * TBLK - 1) // 512)[None].astype(jnp.int32)]
    )
    cross_out = cross_attention(cross_info, cross_q, whole_keys, whole_values)
    return (self_out, cross_out)


def solution(mesh):
    seq = mesh.shape["seq"]
    txt = mesh.shape["txt"]
    inner = Mesh(np.asarray(mesh.devices).reshape(seq // 2, 2, txt), ("chip", "core", "txt"))
    rows = P(("chip", "core"), "txt")
    return jax.shard_map(
        per_device,
        mesh=inner,
        in_specs=(rows, rows, rows, rows, P("txt", None), P("txt", None), P(("chip", "core"))),
        out_specs=(rows, rows),
        check_vma=False,
    )
```

time: 574 us -> 398 us (0.69)
  local copies, waits for them, and re-layouts: 149 us -> 12.9 us
  Pallas kernels: 0 us -> 131 us
  matrix products: 118 us -> 0 us
  loops' own time: 93.5 us -> 0 us
  waiting for transfers between devices: 145 us -> 209 us
  other arithmetic: 42.7 us -> 5.16 us
  starting transfers between devices: 8.81 us -> 20.8 us
    pallas_call x0 -> x3, Pallas kernels: none -> 131 us  [the longest x2 114 us: self_partial(): pl.pallas_call(self_kernel, grid_spec=grid_spec, out_shape=[jax.ShapeDtyp...]
    dot_general x388 -> x0, matrix products: 118 us -> none  [the longest x194 63.3 us: softmax_update(): lax.dot_general(query[:, low:high], keys[:, low:high], (((1,), (1,)), (()...]
    another operation x97 -> x0, loops' own time: 93.5 us -> none  [the longest x1 86.1 us: per_device(): lax.scan(one_block, carry, (key_blocks, value_blocks, jnp.arange(length /...]
    all_gather x2 -> x4, waiting for transfers between devices: 101 us -> 163 us  [the longest x2 84.7 us: per_device(): values = lax.all_gather(self_v[:, cols], 'chip', axis=0, tiled=True)]
    squeeze x48 -> x0, local copies, waits for them, and re-layouts: 51.4 us -> none  [per_device(): lax.scan(one_block, carry, (key_blocks, value_blocks, jnp.arange(length /...]
    slice x193 -> x7, local copies, waits for them, and re-layouts: 53.4 us -> 7.04 us  [the longest x2 1.89 us: per_device(): o_back = lax.ppermute(o_part[rows:], 'core', swap)]
    reduce_sum x97 -> x0, other arithmetic: 36 us -> none  [softmax_update(): sums.append(totals[head] * shrink + jnp.sum(probs, axis=1))]
    dynamic_slice x48 -> x0, local copies, waits for them, and re-layouts: 29.3 us -> none  [per_device(): lax.scan(one_block, carry, (key_blocks, value_blocks, jnp.arange(length /...]
  transfers between devices with their start and end apart: 4 -> 12, of which waited for: 4 -> 6; matrix products, arithmetic and copies ran while one was open for 4% -> 3% of each run, Pallas kernels for 0% -> 33%
where the time goes in v1:
time: 398 us; the launch traced here: 393 us
  waiting for transfers between devices  209 us (53%)
  Pallas kernels  131 us (33%)
  starting transfers between devices  20.8 us (5%)
  between operations  14.6 us (4%)
  local copies, waits for them, and re-layouts  12.9 us (3%)
  other arithmetic  5.16 us (1%)
    pallas_call x2, Pallas kernels, self_partial(): pl.pallas_call(self_kernel, grid_spec=grid_spec, out_shape=[jax.ShapeDtyp...  114 us
    all_gather x2, waiting for transfers between devices, per_device(): values = lax.all_gather(self_v[:, cols], 'chip', axis=0, tiled=True)  84.7 us
    all_gather x2, waiting for transfers between devices, per_device(): keys = lax.all_gather(self_k[:, cols], 'chip', axis=0, tiled=True)  78.6 us
    all_to_all x1, waiting for transfers between devices, per_device(): lax.all_to_all(text_k, 'txt', split_axis=1, concat_axis=0, tiled=True)  24.3 us
    all_to_all x1, waiting for transfers between devices, per_device(): lax.all_to_all(text_v, 'txt', split_axis=1, concat_axis=0, tiled=True)  19.2 us
    pallas_call x1, Pallas kernels, cross_attention(): pl.pallas_call(cross_kernel, grid_spec=grid_spec, out_shape=jax.ShapeDtyp...  16.4 us
    ppermute x2, starting transfers between devices, per_device(): lse_back = lax.ppermute(lse_part[rows:], 'core', swap)  10.3 us
  transfers between devices with their start and end apart: 12, of which 6 were waited for; matrix products, arithmetic and copies ran while one was open for 3% of the time, Pallas kernels for 33%

profile of v1, /device:TPU:249, one launch (start us, length us, event | category | flops | bytes accessed | tf_op | source)
XLA Modules:
  0.0 393.3 jit_solution(7705634032415645930)
XLA Ops:
  7.2 0.0 all-gather.5.cloned.1.call-start
  7.2 1.6 fusion.5
  8.8 0.0 all-gather.5.cloned.1.call-update
  8.9 0.0 all-gather.7.cloned.1.call-start
  8.9 1.6 fusion.4
  10.5 0.0 all-gather.7.cloned.1.call-update
  10.6 0.0 all-gather.11.cloned.1.call-start
  10.6 0.7 all-gather.11.cloned.1.call-update
  11.3 0.0 all-gather.9.cloned.1.call-start
  11.4 0.5 all-gather.9.cloned.1.call-update
  11.9 3.1 copy.16
  15.0 4.6 %all-to-all-start = ((bf16[1024,4,256]{2,0,1:T(8,128)(2,1)}), bf16[1024,4,256]{2,0,1:T(8,128)(2,1)}, u32[]{:S(2)}, u32[]{:S(2)}) async-start(bf16[1024,4,256]{2,0,1:T(8,128)(2,1)} %bitcast.17), calls=%async_computation | async-start | bytes 4194304 | tf_op jit(solution)/shard_map/all_to_all | solution.py:198
  19.6 1.5 copy.15
  21.1 24.3 %all-to-all-done = bf16[1024,4,256]{2,0,1:T(8,128)(2,1)} async-done(((bf16[1024,4,256]{2,0,1:T(8,128)(2,1)}), bf16[1024,4,256]{2,0,1:T(8,128)(2,1)}, u32[]{:S(2)}, u32[]{:S(2)}) %all-to-all-start) | async-done | bytes 2097184 | tf_op jit(solution)/shard_map/all_to_all | solution.py:198
  45.4 3.7 all-to-all-start.1
  49.2 1.6 collective-permute-start
  50.8 0.1 collective-permute-start.3
  50.9 0.6 reduce_max.9
  52.3 0.6 pad_add_fusion.1.info_ref
  52.8 0.6 pad_add_fusion.info_ref
  53.5 0.0 collective-permute-done
  53.5 0.7 pad_maximum_fusion.q_ref
  54.2 0.0 collective-permute-done.3
  54.2 0.7 pad_maximum_fusion.1.q_ref
  54.9 19.2 %all-to-all-done.1 = bf16[1024,4,256]{2,0,1:T(8,128)(2,1)S(1)} async-done(((bf16[1024,4,256]{2,0,1:T(8,128)(2,1)}), bf16[1024,4,256]{2,0,1:T(8,128)(2,1)S(1)}, u32[]{:S(2)}, u32[]{:S(2)}) %all-to-all-start.1) | async-done | bytes 2097184 | tf_op jit(solution)/shard_map/all_to_all | solution.py:199
  74.0 1.3 copy-done.1
  75.4 16.4 %shard_map.88 = bf16[384,256]{1,0:T(8,128)(2,1)} custom-call(s32[4]{0:T(128)} %pad_add_fusion.1.info_ref, bf16[384,256]{1,0:T(8,128)(2,1)} %q_ref.1, bf16[4096,256]{1,0:T(8,128)(2,1)} %bitcast.5.k_ref, bf16[4096,256]{1,0:T(8,128)(2,1)} %bitcast.20), custom_call_target="tpu_custom_call" | custom-call | flops 1610612736 | bytes 4587520 | tf_op jit(solution)/shard_map/pallas_call | solution.py:170
  91.8 70.2 %all-gather.7.cloned.1.call-done.v_ref = bf16[12288,128]{1,0:T(8,128)(2,1)} async-done(((bf16[384,128]{1,0:T(8,128)(2,1)}), bf16[12288,128]{1,0:T(8,128)(2,1)}) %all-gather.7.cloned.1.call-update) | async-done | bytes 3145744 | tf_op jit(solution)/shard_map/all_gather | solution.py:206
  162.0 57.1 %shard_map.86 = (f32[768,128]{1,0:T(8,128)}, f32[768,128]{1,0:T(8,128)}) custom-call(s32[3]{0:T(128)} %pad_add_fusion.info_ref, bf16[768,128]{1,0:T(8,128)(2,1)} %pad_maximum_fusion.q_ref, bf16[12288,128]{1,0:T(8,128)(2,1)} %all-gather.5.cloned.1.call-done.k_ref, bf16[12288,128]{1,0:T(8,128)(2,1)} %all-gather.7.cloned.1.call-done.v_ref), custom_call_target="tpu_custom_call" | custom-call | flops 2415919104 | bytes 7274496 | tf_op jit(solution)/shard_map/pallas_call | solution.py:104
  219.1 0.9 slice.47
  220.0 5.2 %collective-permute-start.1 = (f32[384,128]{1,0:T(8,128)S(1)}, f32[384,128]{1,0:T(8,128)S(1)}, u32[]{:S(2)}, u32[]{:S(2)}) collective-permute-start(f32[384,128]{1,0:T(8,128)S(1)} %slice.47), channel_id=1, source_target_pairs={{0,4},{4,0},{1,5},{5,1},{2,6},{6,2},{3,7},{7,3},{8,12},{12,8},{9,1... | collective-permute-start | bytes 589832 | tf_op jit(solution)/shard_map/ppermute | solution.py:210
  225.2 0.9 slice.48
  226.1 0.0 copy-start.2
  226.1 0.1 collective-permute-start.2
  226.2 14.5 %all-gather.11.cloned.1.call-done.v_ref = bf16[12288,128]{1,0:T(8,128)(2,1)} async-done(((bf16[384,128]{1,0:T(8,128)(2,1)}), bf16[12288,128]{1,0:T(8,128)(2,1)}) %all-gather.11.cloned.1.call-update) | async-done | bytes 3145744 | tf_op jit(solution)/shard_map/all_gather | solution.py:206
  240.7 78.6 %all-gather.9.cloned.1.call-done.k_ref = bf16[12288,128]{1,0:T(8,128)(2,1)} async-done(((bf16[384,128]{1,0:T(8,128)(2,1)}), bf16[12288,128]{1,0:T(8,128)(2,1)}) %all-gather.9.cloned.1.call-update) | async-done | bytes 3145744 | tf_op jit(solution)/shard_map/all_gather | solution.py:205
  319.3 57.1 %shard_map.87 = (f32[768,128]{1,0:T(8,128)}, f32[768,128]{1,0:T(8,128)}) custom-call(s32[3]{0:T(128)} %pad_add_fusion.info_ref, bf16[768,128]{1,0:T(8,128)(2,1)} %pad_maximum_fusion.1.q_ref, bf16[12288,128]{1,0:T(8,128)(2,1)} %all-gather.9.cloned.1.call-done.k_ref, bf16[12288,128]{1,0:T(8,128)(2,1)} %all-gather.11.cloned.1.call-done.v_ref), custom_call_target="tpu_custom_call" | custom-call | flops 2415919104 | bytes 7274496 | tf_op jit(solution)/shard_map/pallas_call | solution.py:104
  376.3 0.9 slice.54
  377.3 5.2 %collective-permute-start.4 = (f32[384,128]{1,0:T(8,128)S(1)}, f32[384,128]{1,0:T(8,128)S(1)}, u32[]{:S(2)}, u32[]{:S(2)}) collective-permute-start(f32[384,128]{1,0:T(8,128)S(1)} %slice.54), channel_id=1, source_target_pairs={{0,4},{4,0},{1,5},{5,1},{2,6},{6,2},{3,7},{7,3},{8,12},{12,8},{9,1... | collective-permute-start | bytes 589832 | tf_op jit(solution)/shard_map/ppermute | solution.py:210
  382.4 0.9 slice.55
  383.4 0.1 collective-permute-start.5
  383.5 0.0 collective-permute-done.1
  383.5 0.0 collective-permute-done.2
  383.5 0.1 divide_convert_fusion.1
  383.6 0.0 collective-permute-done.4
  383.6 1.3 collective-permute-done.5
  384.9 1.1 divide_convert_fusion
  386.0 0.7 pad_maximum_fusion.2
  (12 shorter events, 0.0 us)
Async XLA Ops:
  7.2 84.6 %all-gather.5.cloned.1.call-start = ((), (), s32[]{:S(2)}) async-start(), calls=%async_computation.2 | async-start | bytes 3244032 | tf_op jit(solution)/shard_map/all_gather | solution.py:205
  8.9 153.1 %all-gather.7.cloned.1.call-start = ((), (), s32[]{:S(2)}) async-start(), calls=%async_computation.3 | async-start | bytes 3244032 | tf_op jit(solution)/shard_map/all_gather | solution.py:206
  10.6 230.1 %all-gather.11.cloned.1.call-start = ((), (), s32[]{:S(2)}) async-start(), calls=%async_computation.5 | async-start | bytes 3244032 | tf_op jit(solution)/shard_map/all_gather | solution.py:206
  11.3 308.0 %all-gather.9.cloned.1.call-start = ((), (), s32[]{:S(2)}) async-start(), calls=%async_computation.4 | async-start | bytes 3244032 | tf_op jit(solution)/shard_map/all_gather | solution.py:205
  15.0 4.7 %copy-start = (bf16[1024,1024]{1,0:T(8,128)(2,1)S(1)}, bf16[1024,1024]{1,0:T(8,128)(2,1)}, u32[]{:S(2)}) copy-start(bf16[1024,1024]{1,0:T(8,128)(2,1)} %param.12) | copy-start | bytes 6291460
  15.0 30.5 %all-to-all-start = ((bf16[1024,4,256]{2,0,1:T(8,128)(2,1)}), bf16[1024,4,256]{2,0,1:T(8,128)(2,1)}, u32[]{:S(2)}, u32[]{:S(2)}) async-start(bf16[1024,4,256]{2,0,1:T(8,128)(2,1)} %bitcast.17), calls=%async_computation | async-start | bytes 4194304 | tf_op jit(solution)/shard_map/all_to_all | solution.py:198
  45.4 3.8 copy-start.4
  45.4 5.5 %copy-start.5 = (s32[3]{0:T(128)S(1)}, s32[3]{0:T(128)}, u32[]{:S(2)}) copy-start(s32[3]{0:T(128)} %param.13) | copy-start | bytes 40
  45.4 28.6 %all-to-all-start.1 = ((bf16[1024,4,256]{2,0,1:T(8,128)(2,1)}), bf16[1024,4,256]{2,0,1:T(8,128)(2,1)S(1)}, u32[]{:S(2)}, u32[]{:S(2)}) async-start(bf16[1024,4,256]{2,0,1:T(8,128)(2,1)} %bitcast.16), calls=%async_computation.1 | async-start | bytes 4194304 | tf_op jit(solution)/shard_map/all_to_all | solution.py:199
  49.2 4.2 %collective-permute-start = (bf16[384,128]{1,0:T(8,128)(2,1)S(1)}, bf16[384,128]{1,0:T(8,128)(2,1)S(1)}, u32[]{:S(2)}, u32[]{:S(2)}) collective-permute-start(bf16[384,128]{1,0:T(8,128)(2,1)S(1)} %get-tuple-element.14), channel_id=1, source_target_pairs={{0,4},{4,0},{1,5},{5,1},{2,6},{6,2},{3,7},{7,3},{8,12},{12,8},{9,1... | collective-permute-start | bytes 294920 | tf_op jit(solution)/shard_map/ppermute | solution.py:207
  50.8 3.3 collective-permute-start.3
  74.0 1.3 copy-start.1
  220.0 163.5 %collective-permute-start.1 = (f32[384,128]{1,0:T(8,128)S(1)}, f32[384,128]{1,0:T(8,128)S(1)}, u32[]{:S(2)}, u32[]{:S(2)}) collective-permute-start(f32[384,128]{1,0:T(8,128)S(1)} %slice.47), channel_id=1, source_target_pairs={{0,4},{4,0},{1,5},{5,1},{2,6},{6,2},{3,7},{7,3},{8,12},{12,8},{9,1... | collective-permute-start | bytes 589832 | tf_op jit(solution)/shard_map/ppermute | solution.py:210
  226.1 157.4 %copy-start.2 = (f32[768,128]{1,0:T(8,128)S(1)}, f32[768,128]{1,0:T(8,128)}, u32[]{:S(2)}) copy-start(f32[768,128]{1,0:T(8,128)} %get-tuple-element.6) | copy-start | bytes 1179652
  226.1 157.4 %copy-start.3 = (f32[768,128]{1,0:T(8,128)S(1)}, f32[768,128]{1,0:T(8,128)}, u32[]{:S(2)}) copy-start(f32[768,128]{1,0:T(8,128)} %get-tuple-element.7) | copy-start | bytes 1179652
  226.1 157.3 %collective-permute-start.2 = (f32[384,128]{1,0:T(8,128)S(1)}, f32[384,128]{1,0:T(8,128)S(1)}, u32[]{:S(2)}, u32[]{:S(2)}) collective-permute-start(f32[384,128]{1,0:T(8,128)S(1)} %slice.48), channel_id=1, source_target_pairs={{0,4},{4,0},{1,5},{5,1},{2,6},{6,2},{3,7},{7,3},{8,12},{12,8},{9,1... | collective-permute-start | bytes 589832 | tf_op jit(solution)/shard_map/ppermute | solution.py:209
  377.3 6.4 %collective-permute-start.4 = (f32[384,128]{1,0:T(8,128)S(1)}, f32[384,128]{1,0:T(8,128)S(1)}, u32[]{:S(2)}, u32[]{:S(2)}) collective-permute-start(f32[384,128]{1,0:T(8,128)S(1)} %slice.54), channel_id=1, source_target_pairs={{0,4},{4,0},{1,5},{5,1},{2,6},{6,2},{3,7},{7,3},{8,12},{12,8},{9,1... | collective-permute-start | bytes 589832 | tf_op jit(solution)/shard_map/ppermute | solution.py:210
  383.4 1.5 collective-permute-start.5
Sparse Core Ops, SparseCore 0:
  10.5 72.6 all-gather.4
  85.8 76.0 all-gather.6
  164.6 76.1 all-gather.10
  243.1 76.0 all-gather.8

commit v2 on v1

v2 whole, which is shorter than its diff:
```python
import functools
import math

import jax
import jax.numpy as jnp
import numpy as np
from jax import lax
from jax.experimental import pallas as pl
from jax.experimental.pallas import tpu as pltpu
from jax.sharding import Mesh
from jax.sharding import PartitionSpec as P

HSIZE = 128
SPAN = 128
TBLK = 128

NEG_FILL = -1e30
FACTOR = 1.0 / math.sqrt(HSIZE)


def online_step(q, k, v, mask, m_ref, l_ref, acc_ref):
    scores = (
        lax.dot_general(q, k, (((1,), (1,)), ((), ())), preferred_element_type=jnp.float32)
        * FACTOR
    )
    if mask is not None:
        scores = jnp.where(mask, scores, NEG_FILL)
    m_prev = m_ref[...]
    m_next = jnp.maximum(m_prev, jnp.max(scores, axis=1, keepdims=True))
    probs = jnp.exp(scores - m_next[:, 0:1])
    if mask is not None:
        probs = jnp.where(mask, probs, 0.0)
    alpha = jnp.exp(m_prev - m_next)
    l_ref[...] = alpha * l_ref[...] + jnp.sum(probs, axis=1, keepdims=True)
    mixed = jnp.dot(probs.astype(jnp.bfloat16), v, preferred_element_type=jnp.float32)
    acc_ref[...] = acc_ref[...] * alpha + mixed
    m_ref[...] = m_next


def self_kernel(info_ref, q_ref, k_ref, v_ref, o_ref, m_ref, l_ref, acc_ref):
    kb = pl.program_id(0)
    nkb = pl.num_programs(0)
    place = info_ref[0]
    last = info_ref[1]
    rows = q_ref.shape[0]
    tk = k_ref.shape[0]
    heads = q_ref.shape[1] // HSIZE

    @pl.when(kb == 0)
    def _():
        m_ref[...] = jnp.full(m_ref.shape, NEG_FILL, jnp.float32)
        l_ref[...] = jnp.zeros(l_ref.shape, jnp.float32)
        acc_ref[...] = jnp.zeros(acc_ref.shape, jnp.float32)

    def run(mask):
        for h in range(heads):
            cols = slice(h * HSIZE, (h + 1) * HSIZE)
            online_step(
                q_ref[:, cols], k_ref[:, cols], v_ref[:, cols], mask,
                m_ref.at[h], l_ref.at[h], acc_ref.at[h],
            )

    @pl.when(kb < last)
    def _():
        run(None)

    @pl.when(kb == last)
    def _():
        r = lax.broadcasted_iota(jnp.int32, (rows, tk), 0) + place * rows
        j = lax.broadcasted_iota(jnp.int32, (rows, tk), 1) + kb * tk
        run(j <= r)

    @pl.when(kb == nkb - 1)
    def _():
        for h in range(heads):
            o_ref[:, h * HSIZE:(h + 1) * HSIZE] = (acc_ref[h] / l_ref[h]).astype(o_ref.dtype)


def self_attention(info, query, kv, tk):
    rows, width = query.shape
    heads = width // HSIZE
    nkb = kv.shape[0] // tk

    def k_map(kb, info_ref):
        return (jnp.minimum(kb, info_ref[1]), 0)

    def v_map(kb, info_ref):
        return (jnp.minimum(kb, info_ref[1]), 1)

    grid_spec = pltpu.PrefetchScalarGridSpec(
        num_scalar_prefetch=1,
        grid=(nkb,),
        in_specs=[
            pl.BlockSpec((rows, width), lambda kb, info_ref: (0, 0)),
            pl.BlockSpec((tk, width), k_map),
            pl.BlockSpec((tk, width), v_map),
        ],
        out_specs=pl.BlockSpec((rows, width), lambda kb, info_ref: (0, 0)),
        scratch_shapes=[
            pltpu.VMEM((heads, rows, HSIZE), jnp.float32),
            pltpu.VMEM((heads, rows, HSIZE), jnp.float32),
            pltpu.VMEM((heads, rows, HSIZE), jnp.float32),
        ],
    )
    keys = kv.shape[0]
    return pl.pallas_call(
        self_kernel,
        grid_spec=grid_spec,
        out_shape=jax.ShapeDtypeStruct(query.shape, jnp.bfloat16),
        compiler_params=pltpu.CompilerParams(dimension_semantics=("arbitrary",)),
        cost_estimate=pl.CostEstimate(
            flops=2 * rows * keys * width,
            transcendentals=rows * keys * heads // 2,
            bytes_accessed=kv.size + query.size * 4,
        ),
    )(info, query, kv, kv)


def cross_kernel(info_ref, q_ref, k_ref, v_ref, o_ref, m_ref, l_ref, acc_ref):
    kb = pl.program_id(1)
    nkb = pl.num_programs(1)
    tk = k_ref.shape[0]
    rows = q_ref.shape[0]
    last = info_ref[3]

    @pl.when(kb == 0)
    def _():
        m_ref[...] = jnp.full(m_ref.shape, NEG_FILL, jnp.float32)
        l_ref[...] = jnp.zeros(l_ref.shape, jnp.float32)
        acc_ref[...] = jnp.zeros(acc_ref.shape, jnp.float32)

    @pl.when(kb <= last)
    def _():
        r = lax.broadcasted_iota(jnp.int32, (rows, tk), 0)
        j = lax.broadcasted_iota(jnp.int32, (rows, tk), 1) + kb * tk
        span = r // SPAN
        limit = jnp.where(span == 0, info_ref[0], jnp.where(span == 1, info_ref[1], info_ref[2]))
        online_step(q_ref[...], k_ref[...], v_ref[...], j < limit * TBLK, m_ref, l_ref, acc_ref)

    @pl.when(kb == nkb - 1)
    def _():
        o_ref[...] = (acc_ref[...] / l_ref[...]).astype(o_ref.dtype)


def cross_attention(info, query, keys, values):
    rows = query.shape[0]
    heads = query.shape[1] // HSIZE
    tk = 512
    nkb = keys.shape[0] // tk

    def kv_map(h, kb, info_ref):
        return (jnp.minimum(kb, info_ref[3]), h)

    grid_spec = pltpu.PrefetchScalarGridSpec(
        num_scalar_prefetch=1,
        grid=(heads, nkb),
        in_specs=[
            pl.BlockSpec((rows, HSIZE), lambda h, kb, info_ref: (0, h)),
            pl.BlockSpec((tk, HSIZE), kv_map),
            pl.BlockSpec((tk, HSIZE), kv_map),
        ],
        out_specs=pl.BlockSpec((rows, HSIZE), lambda h, kb, info_ref: (0, h)),
        scratch_shapes=[
            pltpu.VMEM((rows, HSIZE), jnp.float32),
            pltpu.VMEM((rows, HSIZE), jnp.float32),
            pltpu.VMEM((rows, HSIZE), jnp.float32),
        ],
    )
    return pl.pallas_call(
        cross_kernel,
        grid_spec=grid_spec,
        out_shape=jax.ShapeDtypeStruct(query.shape, jnp.bfloat16),
        compiler_params=pltpu.CompilerParams(dimension_semantics=("arbitrary", "arbitrary")),
        cost_estimate=pl.CostEstimate(
            flops=4 * rows * keys.shape[0] * query.shape[1],
            transcendentals=rows * keys.shape[0] * heads,
            bytes_accessed=keys.size * 2 + values.size * 2 + query.size * 4,
        ),
    )(info, query, keys, values)


def per_device(self_q, self_k, self_v, cross_q, text_k, text_v, lags):
    rows = self_q.shape[0]
    tk = 2 * rows
    place = lax.axis_index("seq")

    whole_keys = lax.all_to_all(text_k, "txt", split_axis=1, concat_axis=0, tiled=True)
    whole_values = lax.all_to_all(text_v, "txt", split_axis=1, concat_axis=0, tiled=True)

    kv = lax.all_gather(jnp.concatenate([self_k, self_v], axis=1), "seq", axis=0, tiled=True)
    info = jnp.stack([place, (place * rows + rows - 1) // tk]).astype(jnp.int32)
    self_out = self_attention(info, self_q, kv, tk)

    top = jnp.max(lags)
    cross_info = jnp.concatenate(
        [lags.astype(jnp.int32), ((top * TBLK - 1) // 512)[None].astype(jnp.int32)]
    )
    cross_out = cross_attention(cross_info, cross_q, whole_keys, whole_values)
    return (self_out, cross_out)


def solution(mesh):
    rows = P("seq", "txt")
    return jax.shard_map(
        per_device,
        mesh=mesh,
        in_specs=(rows, rows, rows, rows, P("txt", None), P("txt", None), P("seq")),
        out_specs=(rows, rows),
        check_vma=False,
    )
```

time: 398 us -> 195 us (0.49); the launches traced: 393 us -> 194 us
  waiting for transfers between devices: 209 us -> 85.6 us
  Pallas kernels: 131 us -> 76.3 us
  starting transfers between devices: 20.8 us -> 8.39 us
  local copies, waits for them, and re-layouts: 12.9 us -> 5.85 us
    all_gather x4 -> x1, waiting for transfers between devices: 163 us -> 38.9 us  [per_device(): lax.all_gather(jnp.concatenate([self_k, self_v], axis=1), 'seq', axis=0,...]
    pallas_call x2 -> x1, Pallas kernels: 114 us -> 59.6 us  [self_attention(): pl.pallas_call(self_kernel, grid_spec=grid_spec, out_shape=jax.ShapeDtype...]
    ppermute x6 -> x0, starting transfers between devices: 12.2 us -> none  [the longest x2 10.3 us: per_device(): lse_back = lax.ppermute(lse_part[rows:], 'core', swap)]
    slice x7 -> x0, local copies, waits for them, and re-layouts: 7.04 us -> none  [the longest x2 1.89 us: per_device(): o_back = lax.ppermute(o_part[rows:], 'core', swap)]
  transfers between devices with their start and end apart: 12 -> 3, of which waited for: 6 -> 3; matrix products, arithmetic and copies ran while one was open for 3% -> 3% of each run, Pallas kernels for 33% -> 9%
where the time goes in v2:
time: 195 us; the launch traced here: 194 us
  waiting for transfers between devices  85.6 us (44%)
  Pallas kernels  76.3 us (39%)
  between operations  14.8 us (8%)
  starting transfers between devices  8.39 us (4%)
  local copies, waits for them, and re-layouts  5.85 us (3%)
  other arithmetic  3.59 us (2%)
    pallas_call x1, Pallas kernels, self_attention(): pl.pallas_call(self_kernel, grid_spec=grid_spec, out_shape=jax.ShapeDtype...  59.6 us
    all_gather x1, waiting for transfers between devices, per_device(): lax.all_gather(jnp.concatenate([self_k, self_v], axis=1), 'seq', axis=0,...  38.9 us
    all_to_all x1, waiting for transfers between devices, per_device(): lax.all_to_all(text_k, 'txt', split_axis=1, concat_axis=0, tiled=True)  24.3 us
    all_to_all x1, waiting for transfers between devices, per_device(): lax.all_to_all(text_v, 'txt', split_axis=1, concat_axis=0, tiled=True)  22.4 us
    pallas_call x1, Pallas kernels, cross_attention(): pl.pallas_call(cross_kernel, grid_spec=grid_spec, out_shape=jax.ShapeDtyp...  16.6 us
    all_to_all x1, starting transfers between devices, per_device(): lax.all_to_all(text_k, 'txt', split_axis=1, concat_axis=0, tiled=True)  4.62 us
  transfers between devices with their start and end apart: 3, of which 3 were waited for; matrix products, arithmetic and copies ran while one was open for 3% of the time, Pallas kernels for 9%

profile of v2, /device:TPU:249, one launch (start us, length us, event | category | flops | bytes accessed | tf_op | source)
XLA Modules:
  0.0 194.5 jit_solution(13150860428420286840)
XLA Ops:
  7.2 0.0 all-gather.2.cloned.1.call-start
  7.2 1.8 pad_maximum_fusion
  9.0 0.0 all-gather.2.cloned.1.call-update
  9.0 3.1 %copy.16 = bf16[128,4,8,256]{3,2,0,1:T(8,128)(2,1)} copy(bf16[128,4,8,256]{3,2,1,0:T(8,128)(2,1)} %bitcast.17) | data formatting | bytes 4194304 | tf_op jit(solution)/shard_map/all_to_all | solution.py:187
  12.1 0.0 copy-start
  12.1 4.6 %all-to-all-start = ((bf16[1024,4,256]{2,0,1:T(8,128)(2,1)}), bf16[1024,4,256]{2,0,1:T(8,128)(2,1)}, u32[]{:S(2)}, u32[]{:S(2)}) async-start(bf16[1024,4,256]{2,0,1:T(8,128)(2,1)} %bitcast.16), calls=%async_computation | async-start | bytes 4194304 | tf_op jit(solution)/shard_map/all_to_all | solution.py:187
  16.7 0.0 copy-done
  16.7 1.5 copy.15
  18.2 24.3 %all-to-all-done = bf16[1024,4,256]{2,0,1:T(8,128)(2,1)} async-done(((bf16[1024,4,256]{2,0,1:T(8,128)(2,1)}), bf16[1024,4,256]{2,0,1:T(8,128)(2,1)}, u32[]{:S(2)}, u32[]{:S(2)}) %all-to-all-start) | async-done | bytes 2097184 | tf_op jit(solution)/shard_map/all_to_all | solution.py:187
  42.5 0.0 copy-start.2
  42.5 3.7 %all-to-all-start.1 = ((bf16[1024,4,256]{2,0,1:T(8,128)(2,1)}), bf16[1024,4,256]{2,0,1:T(8,128)(2,1)S(1)}, u32[]{:S(2)}, u32[]{:S(2)}) async-start(bf16[1024,4,256]{2,0,1:T(8,128)(2,1)} %bitcast.15), calls=%async_computation.1 | async-start | bytes 4194304 | tf_op jit(solution)/shard_map/all_to_all | solution.py:188
  46.3 0.0 copy-done.2
  46.3 0.6 reduce_max.9
  47.6 0.6 pad_add_fusion.1.info_ref
  48.2 0.6 pad_add_fusion.info_ref
  48.8 22.4 %all-to-all-done.1 = bf16[1024,4,256]{2,0,1:T(8,128)(2,1)S(1)} async-done(((bf16[1024,4,256]{2,0,1:T(8,128)(2,1)}), bf16[1024,4,256]{2,0,1:T(8,128)(2,1)S(1)}, u32[]{:S(2)}, u32[]{:S(2)}) %all-to-all-start.1) | async-done | bytes 2097184 | tf_op jit(solution)/shard_map/all_to_all | solution.py:188
  71.1 0.0 copy-start.1
  71.1 1.3 copy-done.1
  72.5 16.6 %shard_map.87 = bf16[384,256]{1,0:T(8,128)(2,1)} custom-call(s32[4]{0:T(128)} %pad_add_fusion.1.info_ref, bf16[384,256]{1,0:T(8,128)(2,1)} %q_ref.3, bf16[4096,256]{1,0:T(8,128)(2,1)} %bitcast.4.k_ref, bf16[4096,256]{1,0:T(8,128)(2,1)} %bitcast.19), custom_call_target="tpu_custom_call" | custom-call | flops 1610612736 | bytes 4587520 | tf_op jit(solution)/shard_map/pallas_call | solution.py:169
  89.1 38.9 %all-gather.2.cloned.1.call-done.k_ref.v_ref = bf16[24576,512]{1,0:T(8,128)(2,1)} async-done(((bf16[384,512]{1,0:T(8,128)(2,1)}), bf16[24576,512]{1,0:T(8,128)(2,1)}) %all-gather.2.cloned.1.call-update) | async-done | bytes 25165840 | tf_op jit(solution)/shard_map/all_gather | solution.py:190
  128.0 59.6 %shard_map.86 = bf16[384,256]{1,0:T(8,128)(2,1)} custom-call(s32[2]{0:T(128)} %pad_add_fusion.info_ref, bf16[384,256]{1,0:T(8,128)(2,1)} %q_ref.2, bf16[24576,512]{1,0:T(8,128)(2,1)} %all-gather.2.cloned.1.call-done.k_ref.v_ref, bf16[24576,512]{1,0:T(8,128)(2,1)} %all-gather.2.cloned.1.call-done.k_ref.v_ref), custom_call_target="tpu_custom_call" | custom-call | flops 4831838208 | bytes 12976128 | tf_op jit(solution)/shard_map/pallas_call | solution.py:106
Async XLA Ops:
  7.2 120.8 %all-gather.2.cloned.1.call-start = ((), (), s32[]{:S(2)}) async-start(), calls=%async_computation.2 | async-start | bytes 25559040 | tf_op jit(solution)/shard_map/all_gather | solution.py:190
  12.1 4.6 %copy-start = (bf16[1024,1024]{1,0:T(8,128)(2,1)S(1)}, bf16[1024,1024]{1,0:T(8,128)(2,1)}, u32[]{:S(2)}) copy-start(bf16[1024,1024]{1,0:T(8,128)(2,1)} %param.12) | copy-start | bytes 6291460
  12.1 30.4 %all-to-all-start = ((bf16[1024,4,256]{2,0,1:T(8,128)(2,1)}), bf16[1024,4,256]{2,0,1:T(8,128)(2,1)}, u32[]{:S(2)}, u32[]{:S(2)}) async-start(bf16[1024,4,256]{2,0,1:T(8,128)(2,1)} %bitcast.16), calls=%async_computation | async-start | bytes 4194304 | tf_op jit(solution)/shard_map/all_to_all | solution.py:187
  42.5 3.8 %copy-start.2 = (s32[3]{0:T(128)S(1)}, s32[3]{0:T(128)}, u32[]{:S(2)}) copy-start(s32[3]{0:T(128)} %param.13) | copy-start | bytes 40
  42.5 28.6 %all-to-all-start.1 = ((bf16[1024,4,256]{2,0,1:T(8,128)(2,1)}), bf16[1024,4,256]{2,0,1:T(8,128)(2,1)S(1)}, u32[]{:S(2)}, u32[]{:S(2)}) async-start(bf16[1024,4,256]{2,0,1:T(8,128)(2,1)} %bitcast.15), calls=%async_computation.1 | async-start | bytes 4194304 | tf_op jit(solution)/shard_map/all_to_all | solution.py:188
  71.1 1.3 copy-start.1
Sparse Core Ops, SparseCore 0:
  10.7 117.2 all-gather.1

commit v3 on v2

--- a/solution.py
+++ b/solution.py
@@ -37,14 +37,18 @@
     m_ref[...] = m_next
 
 
-def self_kernel(info_ref, q_ref, k_ref, v_ref, o_ref, m_ref, l_ref, acc_ref):
+def self_kernel(info_ref, q_ref, k_ref, v_ref, o_ref, lse_ref, m_ref, l_ref, acc_ref):
     kb = pl.program_id(0)
     nkb = pl.num_programs(0)
-    place = info_ref[0]
-    last = info_ref[1]
+    qblk = info_ref[0]
+    lo = info_ref[1]
+    hi = info_ref[2]
+    base = info_ref[3]
+    top = info_ref[4]
     rows = q_ref.shape[0]
     tk = k_ref.shape[0]
     heads = q_ref.shape[1] // HSIZE
+    blk = base + kb
 
     @pl.when(kb == 0)
     def _():
@@ -60,60 +64,84 @@
                 m_ref.at[h], l_ref.at[h], acc_ref.at[h],
             )
 
-    @pl.when(kb < last)
+    live = blk <= top
+    edge = jnp.logical_or(blk == base, blk == top)
+
+    @pl.when(jnp.logical_and(live, jnp.logical_not(edge)))
     def _():
         run(None)
 
-    @pl.when(kb == last)
-    def _():
-        r = lax.broadcasted_iota(jnp.int32, (rows, tk), 0) + place * rows
-        j = lax.broadcasted_iota(jnp.int32, (rows, tk), 1) + kb * tk
-        run(j <= r)
+    @pl.when(jnp.logical_and(live, edge))
+    def _():
+        r = lax.broadcasted_iota(jnp.int32, (rows, tk), 0) + qblk * rows
+        j = lax.broadcasted_iota(jnp.int32, (rows, tk), 1) + blk * tk
+        inside = jnp.logical_and(j >= lo * rows, j < hi * rows)
+        run(jnp.logical_and(j <= r, inside))
 
     @pl.when(kb == nkb - 1)
     def _():
         for h in range(heads):
-            o_ref[:, h * HSIZE:(h + 1) * HSIZE] = (acc_ref[h] / l_ref[h]).astype(o_ref.dtype)
-
-
-def self_attention(info, query, kv, tk):
+            l = l_ref[h]
+            seen = l > 0.0
+            safe = jnp.where(seen, l, 1.0)
+            o_ref[:, h * HSIZE:(h + 1) * HSIZE] = acc_ref[h] / safe
+            lse_ref[h] = jnp.where(seen, m_ref[h] + jnp.log(safe), NEG_FILL)
+
+
+def self_partial(qblk, lo, hi, query, kv, tk, steps):
     rows, width = query.shape
     heads = width // HSIZE
-    nkb = kv.shape[0] // tk
+    per = tk // rows
+    base = lo // per
+    top = jnp.where(hi > lo, (hi - 1) // per, base - 1)
+    info = jnp.stack([qblk, lo, hi, base, top, jnp.maximum(top, base)]).astype(jnp.int32)
 
     def k_map(kb, info_ref):
-        return (jnp.minimum(kb, info_ref[1]), 0)
+        return (jnp.minimum(info_ref[3] + kb, info_ref[5]), 0)
 
     def v_map(kb, info_ref):
-        return (jnp.minimum(kb, info_ref[1]), 1)
+        return (jnp.minimum(info_ref[3] + kb, info_ref[5]), 1)
 
     grid_spec = pltpu.PrefetchScalarGridSpec(
         num_scalar_prefetch=1,
-        grid=(nkb,),
+        grid=(steps,),
         in_specs=[
             pl.BlockSpec((rows, width), lambda kb, info_ref: (0, 0)),
             pl.BlockSpec((tk, width), k_map),
             pl.BlockSpec((tk, width), v_map),
         ],
-        out_specs=pl.BlockSpec((rows, width), lambda kb, info_ref: (0, 0)),
+        out_specs=[
+            pl.BlockSpec((rows, width), lambda kb, info_ref: (0, 0)),
+            pl.BlockSpec((heads, rows, HSIZE), lambda kb, info_ref: (0, 0, 0)),
+        ],
         scratch_shapes=[
             pltpu.VMEM((heads, rows, HSIZE), jnp.float32),
             pltpu.VMEM((heads, rows, HSIZE), jnp.float32),
             pltpu.VMEM((heads, rows, HSIZE), jnp.float32),
         ],
     )
-    keys = kv.shape[0]
+    keys = steps * tk
     return pl.pallas_call(
         self_kernel,
         grid_spec=grid_spec,
-        out_shape=jax.ShapeDtypeStruct(query.shape, jnp.bfloat16),
+        out_shape=[
+            jax.ShapeDtypeStruct((rows, width), jnp.float32),
+            jax.ShapeDtypeStruct((heads, rows, HSIZE), jnp.float32),
+        ],
         compiler_params=pltpu.CompilerParams(dimension_semantics=("arbitrary",)),
         cost_estimate=pl.CostEstimate(
             flops=2 * rows * keys * width,
-            transcendentals=rows * keys * heads // 2,
-            bytes_accessed=kv.size + query.size * 4,
+            transcendentals=rows * keys * heads,
+            bytes_accessed=keys * width * 4 + query.size * 2 + rows * width * 8,
         ),
     )(info, query, kv, kv)
+
+
+def spread(lse):
+    heads, rows, _ = lse.shape
+    return jnp.broadcast_to(jnp.transpose(lse, (1, 0, 2)), (rows, heads, HSIZE)).reshape(
+        rows, heads * HSIZE
+    )
 
 
 def cross_kernel(info_ref, q_ref, k_ref, v_ref, o_ref, m_ref, l_ref, acc_ref):
@@ -188,8 +216,26 @@
     whole_values = lax.all_to_all(text_v, "txt", split_axis=1, concat_axis=0, tiled=True)
 
     kv = lax.all_gather(jnp.concatenate([self_k, self_v], axis=1), "seq", axis=0, tiled=True)
-    info = jnp.stack([place, (place * rows + rows - 1) // tk]).astype(jnp.int32)
-    self_out = self_attention(info, self_q, kv, tk)
+    blocks = kv.shape[0] // rows
+    half = blocks // 2
+    pairs = [(i, blocks - 1 - i) for i in range(blocks)]
+    partner = blocks - 1 - place
+    heavy = place >= half
+    other_q = lax.ppermute(self_q, "seq", pairs)
+
+    b_hi = jnp.where(heavy, 0, half - 1 - place)
+    o_b, lse_b = self_partial(partner, 0, b_hi, other_q, kv, tk, half // 2)
+    o_back = lax.ppermute(o_b, "seq", pairs)
+    lse_back = lax.ppermute(lse_b[:, :, :1], "seq", pairs)
+
+    a_lo = jnp.where(heavy, place - half, 0)
+    o_a, lse_a = self_partial(place, a_lo, place + 1, self_q, kv, tk, (half + 1) // 2 + 1)
+    la = spread(lse_a[:, :, :1])
+    lb = spread(lse_back)
+    peak = jnp.maximum(la, lb)
+    w_a = jnp.exp(la - peak)
+    w_b = jnp.exp(lb - peak)
+    self_out = ((o_a * w_a + o_back * w_b) / (w_a + w_b)).astype(jnp.bfloat16)
 
     top = jnp.max(lags)
     cross_info = jnp.concatenate(

time: 195 us -> 220 us (1.13)
  the two profiles are of different devices: /device:TPU:249 before, /device:TPU:1 now
where the time goes in v3:
time: 220 us; the launch traced here: 219 us
  waiting for transfers between devices  119 us (54%)
  Pallas kernels  42.1 us (19%)
  starting transfers between devices  25.6 us (12%)
  between operations  14.7 us (7%)
  local copies, waits for them, and re-layouts  13.9 us (6%)
  other arithmetic  3.94 us (2%)
    all_gather x1, waiting for transfers between devices, per_device(): lax.all_gather(jnp.concatenate([self_k, self_v], axis=1), 'seq', axis=0,...  64 us
    pallas_call x2, Pallas kernels, self_partial(): pl.pallas_call(self_kernel, grid_spec=grid_spec, out_shape=[jax.ShapeDtyp...  35.9 us
    ppermute x1, waiting for transfers between devices, per_device(): lse_back = lax.ppermute(lse_b[:, :, :1], 'seq', pairs)  24.4 us
    all_to_all x1, waiting for transfers between devices, per_device(): lax.all_to_all(text_k, 'txt', split_axis=1, concat_axis=0, tiled=True)  22.6 us
    ppermute x1, starting transfers between devices, per_device(): other_q = lax.ppermute(self_q, 'seq', pairs)  11.7 us
    all_to_all x1, waiting for transfers between devices, per_device(): lax.all_to_all(text_v, 'txt', split_axis=1, concat_axis=0, tiled=True)  7.85 us
    pallas_call x1, Pallas kernels, cross_attention(): pl.pallas_call(cross_kernel, grid_spec=grid_spec, out_shape=jax.ShapeDtyp...  6.12 us
    broadcast_in_dim x4, local copies, waits for them, and re-layouts, spread(): jnp.broadcast_to(jnp.transpose(lse, (1, 0, 2)), (rows, heads, HSIZE))  5.67 us
  transfers between devices with their start and end apart: 6, of which 4 were waited for; matrix products, arithmetic and copies ran while one was open for 6% of the time, Pallas kernels for 5%

profile of v3, /device:TPU:1, one launch (start us, length us, event | category | flops | bytes accessed | tf_op | source)
XLA Modules:
  0.0 219.1 jit_solution(7842868632135676588)
XLA Ops:
  7.2 0.0 all-gather.2.cloned.1.call-start
  7.2 1.8 pad_maximum_fusion
  9.0 0.0 all-gather.2.cloned.1.call-update
  9.0 3.1 %copy.28 = bf16[128,4,8,256]{3,2,0,1:T(8,128)(2,1)} copy(bf16[128,4,8,256]{3,2,1,0:T(8,128)(2,1)} %bitcast.47) | data formatting | bytes 4194304 | tf_op jit(solution)/shard_map/all_to_all | solution.py:215
  12.1 0.0 copy-start
  12.1 5.0 %all-to-all-start = ((bf16[1024,4,256]{2,0,1:T(8,128)(2,1)}), bf16[1024,4,256]{2,0,1:T(8,128)(2,1)}, u32[]{:S(2)}, u32[]{:S(2)}) async-start(bf16[1024,4,256]{2,0,1:T(8,128)(2,1)} %bitcast.45), calls=%async_computation | async-start | bytes 4194304 | tf_op jit(solution)/shard_map/all_to_all | solution.py:215
  17.1 0.0 copy-done
  17.1 1.5 copy.27
  18.5 22.6 %all-to-all-done = bf16[1024,4,256]{2,0,1:T(8,128)(2,1)} async-done(((bf16[1024,4,256]{2,0,1:T(8,128)(2,1)}), bf16[1024,4,256]{2,0,1:T(8,128)(2,1)}, u32[]{:S(2)}, u32[]{:S(2)}) %all-to-all-start) | async-done | bytes 2097184 | tf_op jit(solution)/shard_map/all_to_all | solution.py:215
  41.1 0.0 copy-start.3
  41.1 0.0 copy-start.5
  41.1 3.7 %all-to-all-start.1 = ((bf16[1024,4,256]{2,0,1:T(8,128)(2,1)}), bf16[1024,4,256]{2,0,1:T(8,128)(2,1)S(1)}, u32[]{:S(2)}, u32[]{:S(2)}) async-start(bf16[1024,4,256]{2,0,1:T(8,128)(2,1)} %bitcast.44), calls=%async_computation.1 | async-start | bytes 4194304 | tf_op jit(solution)/shard_map/all_to_all | solution.py:216
  44.9 0.0 copy-done.3
  44.9 11.7 %collective-permute-start = (bf16[384,256]{1,0:T(8,128)(2,1)S(1)}, bf16[384,256]{1,0:T(8,128)(2,1)S(1)}, u32[]{:S(2)}, u32[]{:S(2)}) collective-permute-start(bf16[384,256]{1,0:T(8,128)(2,1)S(1)} %copy-done.3), channel_id=1, source_target_pairs={{0,252},{4,248},{8,244},{12,240},{16,236},{20,232},{24,228},{28,22... | collective-permute-start | bytes 589832 | tf_op jit(solution)/shard_map/ppermute | solution.py:224
  56.7 0.0 copy-done.5
  56.7 0.6 reduce_max.9
  58.0 0.7 pad_add_fusion.info_ref
  58.6 0.7 stack.47.info_ref
  59.3 0.7 stack.42.info_ref
  60.0 7.8 %all-to-all-done.1 = bf16[1024,4,256]{2,0,1:T(8,128)(2,1)S(1)} async-done(((bf16[1024,4,256]{2,0,1:T(8,128)(2,1)}), bf16[1024,4,256]{2,0,1:T(8,128)(2,1)S(1)}, u32[]{:S(2)}, u32[]{:S(2)}) %all-to-all-start.1) | async-done | bytes 2097184 | tf_op jit(solution)/shard_map/all_to_all | solution.py:216
  67.8 0.0 copy-start.1
  67.8 1.3 copy-done.1
  69.1 6.1 %shard_map.88 = bf16[384,256]{1,0:T(8,128)(2,1)} custom-call(s32[4]{0:T(128)} %pad_add_fusion.info_ref, bf16[384,256]{1,0:T(8,128)(2,1)} %q_ref.3, bf16[4096,256]{1,0:T(8,128)(2,1)} %bitcast.16.k_ref, bf16[4096,256]{1,0:T(8,128)(2,1)} %bitcast.49), custom_call_target="tpu_custom_call" | custom-call | flops 1610612736 | bytes 4587520 | tf_op jit(solution)/shard_map/pallas_call | solution.py:197
  75.3 0.0 collective-permute-done.q_ref
  75.3 0.0 copy-start.4
  75.3 64.0 %all-gather.2.cloned.1.call-done.k_ref.v_ref = bf16[24576,512]{1,0:T(8,128)(2,1)} async-done(((bf16[384,512]{1,0:T(8,128)(2,1)}), bf16[24576,512]{1,0:T(8,128)(2,1)}) %all-gather.2.cloned.1.call-update) | async-done | bytes 25165840 | tf_op jit(solution)/shard_map/all_gather | solution.py:218
  139.2 0.0 copy-done.4
  139.3 30.1 %shard_map.87 = (f32[384,256]{1,0:T(8,128)}, f32[2,384,128]{2,1,0:T(8,128)}) custom-call(s32[6]{0:T(128)} %stack.47.info_ref, bf16[384,256]{1,0:T(8,128)(2,1)} %copy-done.4, bf16[24576,512]{1,0:T(8,128)(2,1)} %all-gather.2.cloned.1.call-done.k_ref.v_ref, bf16[24576,512]{1,0:T(8,128)(2,1)} %all-gather.2.cloned.1.call-done.k_ref.v_ref), custom_call_target="tpu_custom_call" | custom-call | flops 2415919104 | bytes 13565952 | tf_op jit(solution)/shard_map/pallas_call | solution.py:124
  169.4 0.0 collective-permute-start.2
  169.4 5.1 %collective-permute-start.1 = (f32[2,384,1]{2,1,0:T(8,128)}, f32[2,384,1]{2,1,0:T(8,128)S(1)}, u32[]{:S(2)}, u32[]{:S(2)}) collective-permute-start(f32[2,384,1]{2,1,0:T(8,128)} %bitcast.55), channel_id=1, source_target_pairs={{0,252},{4,248},{8,244},{12,240},{16,236},{20,232},{24,228},{28,22... | collective-permute-start | bytes 9224 | tf_op jit(solution)/shard_map/ppermute | solution.py:229
  174.5 5.8 %shard_map.86 = (f32[384,256]{1,0:T(8,128)}, f32[2,384,128]{2,1,0:T(8,128)}) custom-call(s32[6]{0:T(128)} %stack.42.info_ref, bf16[384,256]{1,0:T(8,128)(2,1)} %q_ref.2, bf16[24576,512]{1,0:T(8,128)(2,1)} %all-gather.2.cloned.1.call-done.k_ref.v_ref, bf16[24576,512]{1,0:T(8,128)(2,1)} %all-gather.2.cloned.1.call-done.k_ref.v_ref), custom_call_target="tpu_custom_call" | custom-call | flops 2566914048 | bytes 14352384 | tf_op jit(solution)/shard_map/pallas_call | solution.py:124
  180.3 0.0 copy-start.2
  180.3 1.1 slice_bitcast_fusion
  181.3 2.4 %copy.17 = f32[384,2,1]{1,0,2:T(8,128)S(1)} copy(f32[384,2,1]{2,0,1:T(8,128)S(1)} %slice_bitcast_fusion) | data formatting | bytes 6144 | tf_op jit(solution)/shard_map/broadcast_in_dim | solution.py:142
  183.7 24.4 %collective-permute-done.1 = f32[2,384,1]{2,1,0:T(8,128)S(1)} collective-permute-done((f32[2,384,1]{2,1,0:T(8,128)}, f32[2,384,1]{2,1,0:T(8,128)S(1)}, u32[]{:S(2)}, u32[]{:S(2)}) %collective-permute-start.1) | collective-permute-done | bytes 3104 | tf_op jit(solution)/shard_map/ppermute | solution.py:229
  208.1 2.4 %copy.18 = f32[384,2,1]{1,0,2:T(8,128)S(1)} copy(f32[384,2,1]{2,0,1:T(8,128)S(1)} %bitcast.54) | data formatting | bytes 6144 | tf_op jit(solution)/shard_map/broadcast_in_dim | solution.py:142
  210.5 0.0 collective-permute-done.2
  210.5 0.5 broadcast_in_dim.20
  211.0 0.5 broadcast_in_dim.18
  211.4 0.0 copy-done.2
  211.4 0.9 divide_convert_fusion
Async XLA Ops:
  7.2 132.1 %all-gather.2.cloned.1.call-start = ((), (), s32[]{:S(2)}) async-start(), calls=%async_computation.2 | async-start | bytes 25559040 | tf_op jit(solution)/shard_map/all_gather | solution.py:218
  12.1 5.0 %copy-start = (bf16[1024,1024]{1,0:T(8,128)(2,1)S(1)}, bf16[1024,1024]{1,0:T(8,128)(2,1)}, u32[]{:S(2)}) copy-start(bf16[1024,1024]{1,0:T(8,128)(2,1)} %param.12) | copy-start | bytes 6291460
  12.1 29.0 %all-to-all-start = ((bf16[1024,4,256]{2,0,1:T(8,128)(2,1)}), bf16[1024,4,256]{2,0,1:T(8,128)(2,1)}, u32[]{:S(2)}, u32[]{:S(2)}) async-start(bf16[1024,4,256]{2,0,1:T(8,128)(2,1)} %bitcast.45), calls=%async_computation | async-start | bytes 4194304 | tf_op jit(solution)/shard_map/all_to_all | solution.py:215
  41.1 3.8 %copy-start.3 = (bf16[384,256]{1,0:T(8,128)(2,1)S(1)}, bf16[384,256]{1,0:T(8,128)(2,1)}, u32[]{:S(2)}) copy-start(bf16[384,256]{1,0:T(8,128)(2,1)} %q_ref.2) | copy-start | bytes 589828
  41.1 15.5 %copy-start.5 = (s32[3]{0:T(128)S(1)}, s32[3]{0:T(128)}, u32[]{:S(2)}) copy-start(s32[3]{0:T(128)} %param.13) | copy-start | bytes 40
  41.1 26.7 %all-to-all-start.1 = ((bf16[1024,4,256]{2,0,1:T(8,128)(2,1)}), bf16[1024,4,256]{2,0,1:T(8,128)(2,1)S(1)}, u32[]{:S(2)}, u32[]{:S(2)}) async-start(bf16[1024,4,256]{2,0,1:T(8,128)(2,1)} %bitcast.44), calls=%async_computation.1 | async-start | bytes 4194304 | tf_op jit(solution)/shard_map/all_to_all | solution.py:216
  44.9 30.3 %collective-permute-start = (bf16[384,256]{1,0:T(8,128)(2,1)S(1)}, bf16[384,256]{1,0:T(8,128)(2,1)S(1)}, u32[]{:S(2)}, u32[]{:S(2)}) collective-permute-start(bf16[384,256]{1,0:T(8,128)(2,1)S(1)} %copy-done.3), channel_id=1, source_target_pairs={{0,252},{4,248},{8,244},{12,240},{16,236},{20,232},{24,228},{28,22... | collective-permute-start | bytes 589832 | tf_op jit(solution)/shard_map/ppermute | solution.py:224
  67.8 1.3 copy-start.1
  75.3 64.0 %copy-start.4 = (bf16[384,256]{1,0:T(8,128)(2,1)}, bf16[384,256]{1,0:T(8,128)(2,1)S(1)}, u32[]{:S(2)}) copy-start(bf16[384,256]{1,0:T(8,128)(2,1)S(1)} %collective-permute-done.q_ref) | copy-start | bytes 589828
  169.4 41.1 %collective-permute-start.2 = (f32[384,256]{1,0:T(8,128)}, f32[384,256]{1,0:T(8,128)S(1)}, u32[]{:S(2)}, u32[]{:S(2)}) collective-permute-start(f32[384,256]{1,0:T(8,128)} %get-tuple-element.9), channel_id=1, source_target_pairs={{0,252},{4,248},{8,244},{12,240},{16,236},{20,232},{24,228},{28,22... | collective-permute-start | bytes 1179656 | tf_op jit(solution)/shard_map/ppermute | solution.py:228
  169.4 38.7 %collective-permute-start.1 = (f32[2,384,1]{2,1,0:T(8,128)}, f32[2,384,1]{2,1,0:T(8,128)S(1)}, u32[]{:S(2)}, u32[]{:S(2)}) collective-permute-start(f32[2,384,1]{2,1,0:T(8,128)} %bitcast.55), channel_id=1, source_target_pairs={{0,252},{4,248},{8,244},{12,240},{16,236},{20,232},{24,228},{28,22... | collective-permute-start | bytes 9224 | tf_op jit(solution)/shard_map/ppermute | solution.py:229
  180.3 31.2 %copy-start.2 = (f32[384,256]{1,0:T(8,128)S(1)}, f32[384,256]{1,0:T(8,128)}, u32[]{:S(2)}) copy-start(f32[384,256]{1,0:T(8,128)} %get-tuple-element.6) | copy-start | bytes 1179652
Sparse Core Ops, SparseCore 0:
  10.7 128.4 all-gather.1

commit v4 on v3

--- a/solution.py
+++ b/solution.py
@@ -16,24 +16,26 @@
 
 NEG_FILL = -1e30
 FACTOR = 1.0 / math.sqrt(HSIZE)
+SCALE2 = FACTOR * 1.4426950408889634
 
 
 def online_step(q, k, v, mask, m_ref, l_ref, acc_ref):
     scores = (
         lax.dot_general(q, k, (((1,), (1,)), ((), ())), preferred_element_type=jnp.float32)
-        * FACTOR
+        * SCALE2
     )
     if mask is not None:
         scores = jnp.where(mask, scores, NEG_FILL)
     m_prev = m_ref[...]
     m_next = jnp.maximum(m_prev, jnp.max(scores, axis=1, keepdims=True))
-    probs = jnp.exp(scores - m_next[:, 0:1])
+    probs = jnp.exp2(scores - m_next[:, 0:1])
     if mask is not None:
         probs = jnp.where(mask, probs, 0.0)
-    alpha = jnp.exp(m_prev - m_next)
-    l_ref[...] = alpha * l_ref[...] + jnp.sum(probs, axis=1, keepdims=True)
-    mixed = jnp.dot(probs.astype(jnp.bfloat16), v, preferred_element_type=jnp.float32)
-    acc_ref[...] = acc_ref[...] * alpha + mixed
+    alpha = jnp.exp2(m_prev - m_next)
+    extended = jnp.concatenate([v, jnp.ones_like(v)], axis=1)
+    mixed = jnp.dot(probs.astype(jnp.bfloat16), extended, preferred_element_type=jnp.float32)
+    l_ref[...] = alpha * l_ref[...] + mixed[:, HSIZE:]
+    acc_ref[...] = acc_ref[...] * alpha + mixed[:, :HSIZE]
     m_ref[...] = m_next
 
 
@@ -85,7 +87,7 @@
             seen = l > 0.0
             safe = jnp.where(seen, l, 1.0)
             o_ref[:, h * HSIZE:(h + 1) * HSIZE] = acc_ref[h] / safe
-            lse_ref[h] = jnp.where(seen, m_ref[h] + jnp.log(safe), NEG_FILL)
+            lse_ref[h] = jnp.where(seen, m_ref[h] + jnp.log2(safe), NEG_FILL)
 
 
 def self_partial(qblk, lo, hi, query, kv, tk, steps):
@@ -225,16 +227,16 @@
 
     b_hi = jnp.where(heavy, 0, half - 1 - place)
     o_b, lse_b = self_partial(partner, 0, b_hi, other_q, kv, tk, half // 2)
+    a_lo = jnp.where(heavy, place - half, 0)
+    o_a, lse_a = self_partial(place, a_lo, place + 1, self_q, kv, tk, (half + 1) // 2 + 1)
+    o_a, lse_a, o_b, lse_b = lax.optimization_barrier((o_a, lse_a, o_b, lse_b))
     o_back = lax.ppermute(o_b, "seq", pairs)
     lse_back = lax.ppermute(lse_b[:, :, :1], "seq", pairs)
-
-    a_lo = jnp.where(heavy, place - half, 0)
-    o_a, lse_a = self_partial(place, a_lo, place + 1, self_q, kv, tk, (half + 1) // 2 + 1)
     la = spread(lse_a[:, :, :1])
     lb = spread(lse_back)
     peak = jnp.maximum(la, lb)
-    w_a = jnp.exp(la - peak)
-    w_b = jnp.exp(lb - peak)
+    w_a = jnp.exp2(la - peak)
+    w_b = jnp.exp2(lb - peak)
     self_out = ((o_a * w_a + o_back * w_b) / (w_a + w_b)).astype(jnp.bfloat16)
 
     top = jnp.max(lags)

time: 220 us -> 226 us (1.027)
  starting transfers between devices: 25.6 us -> 37.4 us
  Pallas kernels: 42.1 us -> 38.4 us
    all_gather x1, waiting for transfers between devices: 64 us -> 74.1 us  [per_device(): lax.all_gather(jnp.concatenate([self_k, self_v], axis=1), 'seq', axis=0,...]
    ppermute x1, starting transfers between devices: 5.06 us -> 14 us  [per_device(): lse_back = lax.ppermute(lse_b[:, :, :1], 'seq', pairs)]
    ppermute x1, waiting for transfers between devices: 24.4 us -> 16 us  [per_device(): lse_back = lax.ppermute(lse_b[:, :, :1], 'seq', pairs)]
    all_to_all x1, waiting for transfers between devices: 7.85 us -> 0.01 us  [per_device(): lax.all_to_all(text_v, 'txt', split_axis=1, concat_axis=0, tiled=True)]
    ppermute x1, waiting for transfers between devices: 0.01 us -> 5.22 us  [per_device(): other_q = lax.ppermute(self_q, 'seq', pairs)]
    pallas_call x2, Pallas kernels: 35.9 us -> 31.9 us  [self_partial(): pl.pallas_call(self_kernel, grid_spec=grid_spec, out_shape=[jax.ShapeDtyp...]
    ppermute x1, starting transfers between devices: 0.01 us -> 2.88 us  [per_device(): o_back = lax.ppermute(o_b, 'seq', pairs)]
  transfers between devices with their start and end apart: 6 -> 6, of which waited for: 4 -> 4; matrix products, arithmetic and copies ran while one was open for 6% -> 5% of each run, Pallas kernels for 5% -> 17%
where the time goes in v4:
time: 226 us; the launch traced here: 225 us
  waiting for transfers between devices  118 us (52%)
  Pallas kernels  38.4 us (17%)
  starting transfers between devices  37.4 us (17%)
  between operations  14.8 us (7%)
  local copies, waits for them, and re-layouts  12.8 us (6%)
  other arithmetic  3.94 us (2%)
    all_gather x1, waiting for transfers between devices, per_device(): lax.all_gather(jnp.concatenate([self_k, self_v], axis=1), 'seq', axis=0,...  74.1 us
    pallas_call x2, Pallas kernels, self_partial(): pl.pallas_call(self_kernel, grid_spec=grid_spec, out_shape=[jax.ShapeDtyp...  31.9 us
    all_to_all x1, waiting for transfers between devices, per_device(): lax.all_to_all(text_k, 'txt', split_axis=1, concat_axis=0, tiled=True)  22.6 us
    ppermute x1, waiting for transfers between devices, per_device(): lse_back = lax.ppermute(lse_b[:, :, :1], 'seq', pairs)  16 us
    ppermute x1, starting transfers between devices, per_device(): lse_back = lax.ppermute(lse_b[:, :, :1], 'seq', pairs)  14 us
    ppermute x1, starting transfers between devices, per_device(): other_q = lax.ppermute(self_q, 'seq', pairs)  11.7 us
    pallas_call x1, Pallas kernels, cross_attention(): pl.pallas_call(cross_kernel, grid_spec=grid_spec, out_shape=jax.ShapeDtyp...  6.46 us
    broadcast_in_dim x4, local copies, waits for them, and re-layouts, spread(): jnp.broadcast_to(jnp.transpose(lse, (1, 0, 2)), (rows, heads, HSIZE))  5.67 us
  transfers between devices with their start and end apart: 6, of which 4 were waited for; matrix products, arithmetic and copies ran while one was open for 5% of the time, Pallas kernels for 17%

profile of v4, /device:TPU:1, one launch (start us, length us, event | category | flops | bytes accessed | tf_op | source)
XLA Modules:
  0.0 225.3 jit_solution(16694444977144465074)
XLA Ops:
  7.2 0.0 all-gather.2.cloned.1.call-start
  7.2 1.8 pad_maximum_fusion
  9.0 0.0 all-gather.2.cloned.1.call-update
  9.0 3.1 %copy.28 = bf16[128,4,8,256]{3,2,0,1:T(8,128)(2,1)} copy(bf16[128,4,8,256]{3,2,1,0:T(8,128)(2,1)} %bitcast.47) | data formatting | bytes 4194304 | tf_op jit(solution)/shard_map/all_to_all | solution.py:217
  12.1 0.0 copy-start
  12.1 5.0 %all-to-all-start = ((bf16[1024,4,256]{2,0,1:T(8,128)(2,1)}), bf16[1024,4,256]{2,0,1:T(8,128)(2,1)}, u32[]{:S(2)}, u32[]{:S(2)}) async-start(bf16[1024,4,256]{2,0,1:T(8,128)(2,1)} %bitcast.45), calls=%async_computation | async-start | bytes 4194304 | tf_op jit(solution)/shard_map/all_to_all | solution.py:217
  17.1 0.0 copy-done
  17.1 1.5 copy.27
  18.5 22.6 %all-to-all-done = bf16[1024,4,256]{2,0,1:T(8,128)(2,1)} async-done(((bf16[1024,4,256]{2,0,1:T(8,128)(2,1)}), bf16[1024,4,256]{2,0,1:T(8,128)(2,1)}, u32[]{:S(2)}, u32[]{:S(2)}) %all-to-all-start) | async-done | bytes 2097184 | tf_op jit(solution)/shard_map/all_to_all | solution.py:217
  41.1 0.0 copy-start.4
  41.2 0.0 copy-start.7
  41.2 3.7 %all-to-all-start.1 = ((bf16[1024,4,256]{2,0,1:T(8,128)(2,1)}), bf16[1024,4,256]{2,0,1:T(8,128)(2,1)S(1)}, u32[]{:S(2)}, u32[]{:S(2)}) async-start(bf16[1024,4,256]{2,0,1:T(8,128)(2,1)} %bitcast.44), calls=%async_computation.1 | async-start | bytes 4194304 | tf_op jit(solution)/shard_map/all_to_all | solution.py:218
  44.9 0.0 copy-done.4
  44.9 11.7 %collective-permute-start = (bf16[384,256]{1,0:T(8,128)(2,1)S(1)}, bf16[384,256]{1,0:T(8,128)(2,1)S(1)}, u32[]{:S(2)}, u32[]{:S(2)}) collective-permute-start(bf16[384,256]{1,0:T(8,128)(2,1)S(1)} %copy-done.4), channel_id=1, source_target_pairs={{0,252},{4,248},{8,244},{12,240},{16,236},{20,232},{24,228},{28,22... | collective-permute-start | bytes 589832 | tf_op jit(solution)/shard_map/ppermute | solution.py:226
  56.7 0.0 copy-done.7
  56.7 0.6 reduce_max.9
  58.1 0.6 stack.47.info_ref
  58.7 0.6 stack.42.info_ref
  59.3 0.6 pad_add_fusion.info_ref
  59.9 5.2 %collective-permute-done.q_ref = bf16[384,256]{1,0:T(8,128)(2,1)S(1)} collective-permute-done((bf16[384,256]{1,0:T(8,128)(2,1)S(1)}, bf16[384,256]{1,0:T(8,128)(2,1)S(1)}, u32[]{:S(2)}, u32[]{:S(2)}) %collective-permute-start) | collective-permute-done | bytes 196640 | tf_op jit(solution)/shard_map/ppermute | solution.py:226
  65.1 0.0 copy-start.5
  65.2 74.1 %all-gather.2.cloned.1.call-done.k_ref.v_ref = bf16[24576,512]{1,0:T(8,128)(2,1)} async-done(((bf16[384,512]{1,0:T(8,128)(2,1)}), bf16[24576,512]{1,0:T(8,128)(2,1)}) %all-gather.2.cloned.1.call-update) | async-done | bytes 25165840 | tf_op jit(solution)/shard_map/all_gather | solution.py:220
  139.3 0.0 copy-done.5
  139.3 26.3 %shard_map.87 = (f32[384,256]{1,0:T(8,128)}, f32[2,384,128]{2,1,0:T(8,128)}) custom-call(s32[6]{0:T(128)} %stack.47.info_ref, bf16[384,256]{1,0:T(8,128)(2,1)} %copy-done.5, bf16[24576,512]{1,0:T(8,128)(2,1)} %all-gather.2.cloned.1.call-done.k_ref.v_ref, bf16[24576,512]{1,0:T(8,128)(2,1)} %all-gather.2.cloned.1.call-done.k_ref.v_ref), custom_call_target="tpu_custom_call" | custom-call | flops 2415919104 | bytes 13565952 | tf_op jit(solution)/shard_map/pallas_call | solution.py:126
  165.6 0.0 copy-start.6
  165.6 5.6 %shard_map.86 = (f32[384,256]{1,0:T(8,128)}, f32[2,384,128]{2,1,0:T(8,128)}) custom-call(s32[6]{0:T(128)} %stack.42.info_ref, bf16[384,256]{1,0:T(8,128)(2,1)} %q_ref.2, bf16[24576,512]{1,0:T(8,128)(2,1)} %all-gather.2.cloned.1.call-done.k_ref.v_ref, bf16[24576,512]{1,0:T(8,128)(2,1)} %all-gather.2.cloned.1.call-done.k_ref.v_ref), custom_call_target="tpu_custom_call" | custom-call | flops 2566914048 | bytes 14352384 | tf_op jit(solution)/shard_map/pallas_call | solution.py:126
  171.2 0.0 copy-done.6
  171.2 2.9 %collective-permute-start.2 = (f32[384,256]{1,0:T(8,128)S(1)}, f32[384,256]{1,0:T(8,128)S(1)}, u32[]{:S(2)}, u32[]{:S(2)}) collective-permute-start(f32[384,256]{1,0:T(8,128)S(1)} %copy-done.6), channel_id=1, source_target_pairs={{0,252},{4,248},{8,244},{12,240},{16,236},{20,232},{24,228},{28,22... | collective-permute-start | bytes 1179656 | tf_op jit(solution)/shard_map/ppermute | solution.py:233
  174.1 0.0 all-to-all-done.1
  174.1 0.0 copy-start.1
  174.1 1.3 copy-done.1
  175.4 0.0 copy-start.3
  175.4 6.5 %shard_map.88 = bf16[384,256]{1,0:T(8,128)(2,1)} custom-call(s32[4]{0:T(128)} %pad_add_fusion.info_ref, bf16[384,256]{1,0:T(8,128)(2,1)} %q_ref.3, bf16[4096,256]{1,0:T(8,128)(2,1)} %bitcast.16.k_ref, bf16[4096,256]{1,0:T(8,128)(2,1)} %bitcast.49), custom_call_target="tpu_custom_call" | custom-call | flops 1610612736 | bytes 4587520 | tf_op jit(solution)/shard_map/pallas_call | solution.py:199
  181.9 0.0 copy-start.2
  181.9 14.0 %collective-permute-start.1 = (f32[2,384,1]{2,1,0:T(8,128)}, f32[2,384,1]{2,1,0:T(8,128)S(1)}, u32[]{:S(2)}, u32[]{:S(2)}) collective-permute-start(f32[2,384,1]{2,1,0:T(8,128)} %bitcast.55), channel_id=1, source_target_pairs={{0,252},{4,248},{8,244},{12,240},{16,236},{20,232},{24,228},{28,22... | collective-permute-start | bytes 9224 | tf_op jit(solution)/shard_map/ppermute | solution.py:234
  195.9 0.0 copy-done.3
  195.9 2.4 %copy.17 = f32[384,2,1]{1,0,2:T(8,128)S(1)} copy(f32[384,2,1]{2,0,1:T(8,128)S(1)} %slice_bitcast_fusion) | data formatting | bytes 6144 | tf_op jit(solution)/shard_map/broadcast_in_dim | solution.py:144
  198.3 16.0 %collective-permute-done.1 = f32[2,384,1]{2,1,0:T(8,128)S(1)} collective-permute-done((f32[2,384,1]{2,1,0:T(8,128)}, f32[2,384,1]{2,1,0:T(8,128)S(1)}, u32[]{:S(2)}, u32[]{:S(2)}) %collective-permute-start.1) | collective-permute-done | bytes 3104 | tf_op jit(solution)/shard_map/ppermute | solution.py:234
  214.3 2.4 %copy.18 = f32[384,2,1]{1,0,2:T(8,128)S(1)} copy(f32[384,2,1]{2,0,1:T(8,128)S(1)} %bitcast.54) | data formatting | bytes 6144 | tf_op jit(solution)/shard_map/broadcast_in_dim | solution.py:144
  216.6 0.0 collective-permute-done.2
  216.6 0.5 broadcast_in_dim.20
  217.1 0.5 broadcast_in_dim.18
  217.6 0.0 copy-done.2
  217.6 0.9 divide_convert_fusion
  (1 shorter events, 0.0 us)
Async XLA Ops:
  7.2 132.1 %all-gather.2.cloned.1.call-start = ((), (), s32[]{:S(2)}) async-start(), calls=%async_computation.2 | async-start | bytes 25559040 | tf_op jit(solution)/shard_map/all_gather | solution.py:220
  12.1 5.0 %copy-start = (bf16[1024,1024]{1,0:T(8,128)(2,1)S(1)}, bf16[1024,1024]{1,0:T(8,128)(2,1)}, u32[]{:S(2)}) copy-start(bf16[1024,1024]{1,0:T(8,128)(2,1)} %param.12) | copy-start | bytes 6291460
  12.1 29.0 %all-to-all-start = ((bf16[1024,4,256]{2,0,1:T(8,128)(2,1)}), bf16[1024,4,256]{2,0,1:T(8,128)(2,1)}, u32[]{:S(2)}, u32[]{:S(2)}) async-start(bf16[1024,4,256]{2,0,1:T(8,128)(2,1)} %bitcast.45), calls=%async_computation | async-start | bytes 4194304 | tf_op jit(solution)/shard_map/all_to_all | solution.py:217
  41.1 3.8 %copy-start.4 = (bf16[384,256]{1,0:T(8,128)(2,1)S(1)}, bf16[384,256]{1,0:T(8,128)(2,1)}, u32[]{:S(2)}) copy-start(bf16[384,256]{1,0:T(8,128)(2,1)} %q_ref.2) | copy-start | bytes 589828
  41.2 15.5 %copy-start.7 = (s32[3]{0:T(128)S(1)}, s32[3]{0:T(128)}, u32[]{:S(2)}) copy-start(s32[3]{0:T(128)} %param.13) | copy-start | bytes 40
  41.2 132.9 %all-to-all-start.1 = ((bf16[1024,4,256]{2,0,1:T(8,128)(2,1)}), bf16[1024,4,256]{2,0,1:T(8,128)(2,1)S(1)}, u32[]{:S(2)}, u32[]{:S(2)}) async-start(bf16[1024,4,256]{2,0,1:T(8,128)(2,1)} %bitcast.44), calls=%async_computation.1 | async-start | bytes 4194304 | tf_op jit(solution)/shard_map/all_to_all | solution.py:218
  44.9 20.2 %collective-permute-start = (bf16[384,256]{1,0:T(8,128)(2,1)S(1)}, bf16[384,256]{1,0:T(8,128)(2,1)S(1)}, u32[]{:S(2)}, u32[]{:S(2)}) collective-permute-start(bf16[384,256]{1,0:T(8,128)(2,1)S(1)} %copy-done.4), channel_id=1, source_target_pairs={{0,252},{4,248},{8,244},{12,240},{16,236},{20,232},{24,228},{28,22... | collective-permute-start | bytes 589832 | tf_op jit(solution)/shard_map/ppermute | solution.py:226
  65.1 74.1 %copy-start.5 = (bf16[384,256]{1,0:T(8,128)(2,1)}, bf16[384,256]{1,0:T(8,128)(2,1)S(1)}, u32[]{:S(2)}) copy-start(bf16[384,256]{1,0:T(8,128)(2,1)S(1)} %collective-permute-done.q_ref) | copy-start | bytes 589828
  165.6 5.6 %copy-start.6 = (f32[384,256]{1,0:T(8,128)S(1)}, f32[384,256]{1,0:T(8,128)}, u32[]{:S(2)}) copy-start(f32[384,256]{1,0:T(8,128)} %get-tuple-element.17) | copy-start | bytes 1179652
  171.2 45.4 %collective-permute-start.2 = (f32[384,256]{1,0:T(8,128)S(1)}, f32[384,256]{1,0:T(8,128)S(1)}, u32[]{:S(2)}, u32[]{:S(2)}) collective-permute-start(f32[384,256]{1,0:T(8,128)S(1)} %copy-done.6), channel_id=1, source_target_pairs={{0,252},{4,248},{8,244},{12,240},{16,236},{20,232},{24,228},{28,22... | collective-permute-start | bytes 1179656 | tf_op jit(solution)/shard_map/ppermute | solution.py:233
  174.1 1.3 copy-start.1
  175.4 20.5 %copy-start.3 = (f32[2,384,128]{2,1,0:T(8,128)S(1)}, f32[2,384,128]{2,1,0:T(8,128)}, u32[]{:S(2)}) copy-start(f32[2,384,128]{2,1,0:T(8,128)} %get-tuple-element.15) | copy-start | bytes 1179652
  181.9 35.7 %copy-start.2 = (f32[384,256]{1,0:T(8,128)S(1)}, f32[384,256]{1,0:T(8,128)}, u32[]{:S(2)}) copy-start(f32[384,256]{1,0:T(8,128)} %get-tuple-element.14) | copy-start | bytes 1179652
  181.9 32.4 %collective-permute-start.1 = (f32[2,384,1]{2,1,0:T(8,128)}, f32[2,384,1]{2,1,0:T(8,128)S(1)}, u32[]{:S(2)}, u32[]{:S(2)}) collective-permute-start(f32[2,384,1]{2,1,0:T(8,128)} %bitcast.55), channel_id=1, source_target_pairs={{0,252},{4,248},{8,244},{12,240},{16,236},{20,232},{24,228},{28,22... | collective-permute-start | bytes 9224 | tf_op jit(solution)/shard_map/ppermute | solution.py:234
Sparse Core Ops, SparseCore 0:
  10.7 128.4 all-gather.1

commit v5 on v4

--- a/solution.py
+++ b/solution.py
@@ -217,7 +217,14 @@
     whole_keys = lax.all_to_all(text_k, "txt", split_axis=1, concat_axis=0, tiled=True)
     whole_values = lax.all_to_all(text_v, "txt", split_axis=1, concat_axis=0, tiled=True)
 
+    top = jnp.max(lags)
+    cross_info = jnp.concatenate(
+        [lags.astype(jnp.int32), ((top * TBLK - 1) // 512)[None].astype(jnp.int32)]
+    )
+    cross_out = cross_attention(cross_info, cross_q, whole_keys, whole_values)
+
     kv = lax.all_gather(jnp.concatenate([self_k, self_v], axis=1), "seq", axis=0, tiled=True)
+    kv, cross_out = lax.optimization_barrier((kv, cross_out))
     blocks = kv.shape[0] // rows
     half = blocks // 2
     pairs = [(i, blocks - 1 - i) for i in range(blocks)]
@@ -239,11 +246,6 @@
     w_b = jnp.exp2(lb - peak)
     self_out = ((o_a * w_a + o_back * w_b) / (w_a + w_b)).astype(jnp.bfloat16)
 
-    top = jnp.max(lags)
-    cross_info = jnp.concatenate(
-        [lags.astype(jnp.int32), ((top * TBLK - 1) // 512)[None].astype(jnp.int32)]
-    )
-    cross_out = cross_attention(cross_info, cross_q, whole_keys, whole_values)
     return (self_out, cross_out)
 
 

time: 226 us -> 224 us (level)
  starting transfers between devices: 37.4 us -> 25.5 us
  waiting for transfers between devices: 118 us -> 127 us
    all_to_all x1, waiting for transfers between devices: 0.01 us -> 22.6 us  [per_device(): lax.all_to_all(text_v, 'txt', split_axis=1, concat_axis=0, tiled=True)]
    ppermute x1, waiting for transfers between devices: 16 us -> 32.8 us  [per_device(): lse_back = lax.ppermute(lse_b[:, :, :1], 'seq', pairs)]
    all_to_all x1, waiting for transfers between devices: 22.6 us -> 7.88 us  [per_device(): lax.all_to_all(text_k, 'txt', split_axis=1, concat_axis=0, tiled=True)]
    ppermute x1, starting transfers between devices: 14 us -> 2.18 us  [per_device(): lse_back = lax.ppermute(lse_b[:, :, :1], 'seq', pairs)]
    all_gather x1, waiting for transfers between devices: 74.1 us -> 63.5 us  [per_device(): lax.all_gather(jnp.concatenate([self_k, self_v], axis=1), 'seq', axis=0,...]
    ppermute x1, waiting for transfers between devices: 5.22 us -> 0.01 us  [per_device(): other_q = lax.ppermute(self_q, 'seq', pairs)]
  transfers between devices with their start and end apart: 6 -> 6, of which waited for: 4 -> 4; matrix products, arithmetic and copies ran while one was open for 5% -> 5% of each run, Pallas kernels for 17% -> 5%
where the time goes in v5:
time: 224 us; the launch traced here: 223 us
  waiting for transfers between devices  127 us (57%)
  Pallas kernels  38.3 us (17%)
  starting transfers between devices  25.5 us (11%)
  between operations  14.8 us (7%)
  local copies, waits for them, and re-layouts  13.6 us (6%)
  other arithmetic  3.94 us (2%)
    all_gather x1, waiting for transfers between devices, per_device(): lax.all_gather(jnp.concatenate([self_k, self_v], axis=1), 'seq', axis=0,...  63.5 us
    ppermute x1, waiting for transfers between devices, per_device(): lse_back = lax.ppermute(lse_b[:, :, :1], 'seq', pairs)  32.8 us
    pallas_call x2, Pallas kernels, self_partial(): pl.pallas_call(self_kernel, grid_spec=grid_spec, out_shape=[jax.ShapeDtyp...  31.8 us
    all_to_all x1, waiting for transfers between devices, per_device(): lax.all_to_all(text_v, 'txt', split_axis=1, concat_axis=0, tiled=True)  22.6 us
    ppermute x1, starting transfers between devices, per_device(): other_q = lax.ppermute(self_q, 'seq', pairs)  11.7 us
    all_to_all x1, waiting for transfers between devices, per_device(): lax.all_to_all(text_k, 'txt', split_axis=1, concat_axis=0, tiled=True)  7.88 us
    pallas_call x1, Pallas kernels, cross_attention(): pl.pallas_call(cross_kernel, grid_spec=grid_spec, out_shape=jax.ShapeDtyp...  6.5 us
    broadcast_in_dim x4, local copies, waits for them, and re-layouts, spread(): jnp.broadcast_to(jnp.transpose(lse, (1, 0, 2)), (rows, heads, HSIZE))  5.67 us
  transfers between devices with their start and end apart: 6, of which 4 were waited for; matrix products, arithmetic and copies ran while one was open for 5% of the time, Pallas kernels for 5%

profile of v5, /device:TPU:1, one launch (start us, length us, event | category | flops | bytes accessed | tf_op | source)
XLA Modules:
  0.0 223.1 jit_solution(11536479422182685063)
XLA Ops:
  7.2 0.0 all-gather.2.cloned.1.call-start
  7.2 1.8 pad_maximum_fusion
  9.0 0.0 all-gather.2.cloned.1.call-update
  9.0 3.1 %copy.27 = bf16[128,4,8,256]{3,2,0,1:T(8,128)(2,1)} copy(bf16[128,4,8,256]{3,2,1,0:T(8,128)(2,1)} %bitcast.47) | data formatting | bytes 4194304 | tf_op jit(solution)/shard_map/all_to_all | solution.py:218
  12.1 0.0 copy-start
  12.1 5.0 %all-to-all-start.1 = ((bf16[1024,4,256]{2,0,1:T(8,128)(2,1)}), bf16[1024,4,256]{2,0,1:T(8,128)(2,1)}, u32[]{:S(2)}, u32[]{:S(2)}) async-start(bf16[1024,4,256]{2,0,1:T(8,128)(2,1)} %bitcast.44), calls=%async_computation.1 | async-start | bytes 4194304 | tf_op jit(solution)/shard_map/all_to_all | solution.py:218
  17.1 0.0 copy-done
  17.1 1.5 copy.28
  18.5 22.6 %all-to-all-done.1 = bf16[1024,4,256]{2,0,1:T(8,128)(2,1)} async-done(((bf16[1024,4,256]{2,0,1:T(8,128)(2,1)}), bf16[1024,4,256]{2,0,1:T(8,128)(2,1)}, u32[]{:S(2)}, u32[]{:S(2)}) %all-to-all-start.1) | async-done | bytes 2097184 | tf_op jit(solution)/shard_map/all_to_all | solution.py:218
  41.2 0.0 copy-start.4
  41.2 0.0 copy-start.6
  41.2 3.7 %all-to-all-start = ((bf16[1024,4,256]{2,0,1:T(8,128)(2,1)}), bf16[1024,4,256]{2,0,1:T(8,128)(2,1)S(1)}, u32[]{:S(2)}, u32[]{:S(2)}) async-start(bf16[1024,4,256]{2,0,1:T(8,128)(2,1)} %bitcast.45), calls=%async_computation | async-start | bytes 4194304 | tf_op jit(solution)/shard_map/all_to_all | solution.py:217
  44.9 0.0 copy-done.4
  44.9 11.7 %collective-permute-start = (bf16[384,256]{1,0:T(8,128)(2,1)S(1)}, bf16[384,256]{1,0:T(8,128)(2,1)S(1)}, u32[]{:S(2)}, u32[]{:S(2)}) collective-permute-start(bf16[384,256]{1,0:T(8,128)(2,1)S(1)} %copy-done.4), channel_id=1, source_target_pairs={{0,252},{4,248},{8,244},{12,240},{16,236},{20,232},{24,228},{28,22... | collective-permute-start | bytes 589832 | tf_op jit(solution)/shard_map/ppermute | solution.py:233
  56.7 0.0 copy-done.6
  56.7 0.6 reduce_max.9
  58.1 0.7 stack.47.info_ref
  58.7 0.6 stack.42.info_ref
  59.3 0.6 pad_add_fusion.info_ref
  60.0 7.9 %all-to-all-done = bf16[1024,4,256]{2,0,1:T(8,128)(2,1)S(1)} async-done(((bf16[1024,4,256]{2,0,1:T(8,128)(2,1)}), bf16[1024,4,256]{2,0,1:T(8,128)(2,1)S(1)}, u32[]{:S(2)}, u32[]{:S(2)}) %all-to-all-start) | async-done | bytes 2097184 | tf_op jit(solution)/shard_map/all_to_all | solution.py:217
  67.9 0.0 copy-start.1
  67.9 1.3 copy-done.1
  69.2 6.5 %shard_map.86 = bf16[384,256]{1,0:T(8,128)(2,1)} custom-call(s32[4]{0:T(128)} %pad_add_fusion.info_ref, bf16[384,256]{1,0:T(8,128)(2,1)} %q_ref.2, bf16[4096,256]{1,0:T(8,128)(2,1)} %bitcast.49, bf16[4096,256]{1,0:T(8,128)(2,1)} %bitcast.10.v_ref), custom_call_target="tpu_custom_call" | custom-call | flops 1610612736 | bytes 4587520 | tf_op jit(solution)/shard_map/pallas_call | solution.py:199
  75.7 63.5 %all-gather.2.cloned.1.call-done.k_ref.v_ref = bf16[24576,512]{1,0:T(8,128)(2,1)} async-done(((bf16[384,512]{1,0:T(8,128)(2,1)}), bf16[24576,512]{1,0:T(8,128)(2,1)}) %all-gather.2.cloned.1.call-update) | async-done | bytes 25165840 | tf_op jit(solution)/shard_map/all_gather | solution.py:226
  139.2 5.6 %shard_map.87 = (f32[384,256]{1,0:T(8,128)}, f32[2,384,128]{2,1,0:T(8,128)}) custom-call(s32[6]{0:T(128)} %stack.42.info_ref, bf16[384,256]{1,0:T(8,128)(2,1)} %q_ref.3, bf16[24576,512]{1,0:T(8,128)(2,1)} %all-gather.2.cloned.1.call-done.k_ref.v_ref, bf16[24576,512]{1,0:T(8,128)(2,1)} %all-gather.2.cloned.1.call-done.k_ref.v_ref), custom_call_target="tpu_custom_call" | custom-call | flops 2566914048 | bytes 14352384 | tf_op jit(solution)/shard_map/pallas_call | solution.py:126
  144.8 0.0 copy-start.3
  144.8 0.0 collective-permute-done.q_ref
  144.8 0.0 copy-start.5
  144.8 0.7 copy-done.5
  145.5 26.3 %shard_map.88 = (f32[384,256]{1,0:T(8,128)}, f32[2,384,128]{2,1,0:T(8,128)}) custom-call(s32[6]{0:T(128)} %stack.47.info_ref, bf16[384,256]{1,0:T(8,128)(2,1)} %copy-done.5, bf16[24576,512]{1,0:T(8,128)(2,1)} %all-gather.2.cloned.1.call-done.k_ref.v_ref, bf16[24576,512]{1,0:T(8,128)(2,1)} %all-gather.2.cloned.1.call-done.k_ref.v_ref), custom_call_target="tpu_custom_call" | custom-call | flops 2415919104 | bytes 13565952 | tf_op jit(solution)/shard_map/pallas_call | solution.py:126
  171.8 0.0 copy-start.2
  171.8 2.9 %collective-permute-start.2 = (f32[384,256]{1,0:T(8,128)}, f32[384,256]{1,0:T(8,128)S(1)}, u32[]{:S(2)}, u32[]{:S(2)}) collective-permute-start(f32[384,256]{1,0:T(8,128)} %get-tuple-element.20), channel_id=1, source_target_pairs={{0,252},{4,248},{8,244},{12,240},{16,236},{20,232},{24,228},{28,22... | collective-permute-start | bytes 1179656 | tf_op jit(solution)/shard_map/ppermute | solution.py:240
  174.6 2.2 collective-permute-start.1
  176.8 0.0 copy-done.3
  176.9 2.4 %copy.17 = f32[384,2,1]{1,0,2:T(8,128)S(1)} copy(f32[384,2,1]{2,0,1:T(8,128)S(1)} %slice_bitcast_fusion) | data formatting | bytes 6144 | tf_op jit(solution)/shard_map/broadcast_in_dim | solution.py:144
  179.2 32.8 %collective-permute-done.1 = f32[2,384,1]{2,1,0:T(8,128)S(1)} collective-permute-done((f32[2,384,1]{2,1,0:T(8,128)}, f32[2,384,1]{2,1,0:T(8,128)S(1)}, u32[]{:S(2)}, u32[]{:S(2)}) %collective-permute-start.1) | collective-permute-done | bytes 3104 | tf_op jit(solution)/shard_map/ppermute | solution.py:241
  212.0 2.4 %copy.18 = f32[384,2,1]{1,0,2:T(8,128)S(1)} copy(f32[384,2,1]{2,0,1:T(8,128)S(1)} %bitcast.54) | data formatting | bytes 6144 | tf_op jit(solution)/shard_map/broadcast_in_dim | solution.py:144
  214.4 0.0 collective-permute-done.2
  214.4 0.5 broadcast_in_dim.21
  214.9 0.5 broadcast_in_dim.19
  215.4 0.0 copy-done.2
  215.4 0.9 divide_convert_fusion
  (1 shorter events, 0.0 us)
Async XLA Ops:
  7.2 132.1 %all-gather.2.cloned.1.call-start = ((), (), s32[]{:S(2)}) async-start(), calls=%async_computation.2 | async-start | bytes 25559040 | tf_op jit(solution)/shard_map/all_gather | solution.py:226
  12.1 5.0 %copy-start = (bf16[1024,1024]{1,0:T(8,128)(2,1)S(1)}, bf16[1024,1024]{1,0:T(8,128)(2,1)}, u32[]{:S(2)}) copy-start(bf16[1024,1024]{1,0:T(8,128)(2,1)} %param.11) | copy-start | bytes 6291460
  12.1 29.1 %all-to-all-start.1 = ((bf16[1024,4,256]{2,0,1:T(8,128)(2,1)}), bf16[1024,4,256]{2,0,1:T(8,128)(2,1)}, u32[]{:S(2)}, u32[]{:S(2)}) async-start(bf16[1024,4,256]{2,0,1:T(8,128)(2,1)} %bitcast.44), calls=%async_computation.1 | async-start | bytes 4194304 | tf_op jit(solution)/shard_map/all_to_all | solution.py:218
  41.2 3.8 %copy-start.4 = (bf16[384,256]{1,0:T(8,128)(2,1)S(1)}, bf16[384,256]{1,0:T(8,128)(2,1)}, u32[]{:S(2)}) copy-start(bf16[384,256]{1,0:T(8,128)(2,1)} %q_ref.3) | copy-start | bytes 589828
  41.2 15.5 %copy-start.6 = (s32[3]{0:T(128)S(1)}, s32[3]{0:T(128)}, u32[]{:S(2)}) copy-start(s32[3]{0:T(128)} %param.13) | copy-start | bytes 40
  41.2 26.7 %all-to-all-start = ((bf16[1024,4,256]{2,0,1:T(8,128)(2,1)}), bf16[1024,4,256]{2,0,1:T(8,128)(2,1)S(1)}, u32[]{:S(2)}, u32[]{:S(2)}) async-start(bf16[1024,4,256]{2,0,1:T(8,128)(2,1)} %bitcast.45), calls=%async_computation | async-start | bytes 4194304 | tf_op jit(solution)/shard_map/all_to_all | solution.py:217
  44.9 99.9 %collective-permute-start = (bf16[384,256]{1,0:T(8,128)(2,1)S(1)}, bf16[384,256]{1,0:T(8,128)(2,1)S(1)}, u32[]{:S(2)}, u32[]{:S(2)}) collective-permute-start(bf16[384,256]{1,0:T(8,128)(2,1)S(1)} %copy-done.4), channel_id=1, source_target_pairs={{0,252},{4,248},{8,244},{12,240},{16,236},{20,232},{24,228},{28,22... | collective-permute-start | bytes 589832 | tf_op jit(solution)/shard_map/ppermute | solution.py:233
  67.9 1.3 copy-start.1
  144.8 32.0 %copy-start.3 = (f32[2,384,128]{2,1,0:T(8,128)S(1)}, f32[2,384,128]{2,1,0:T(8,128)}, u32[]{:S(2)}) copy-start(f32[2,384,128]{2,1,0:T(8,128)} %get-tuple-element.18) | copy-start | bytes 1179652
  144.8 0.7 copy-start.5
  171.8 43.6 %copy-start.2 = (f32[384,256]{1,0:T(8,128)S(1)}, f32[384,256]{1,0:T(8,128)}, u32[]{:S(2)}) copy-start(f32[384,256]{1,0:T(8,128)} %get-tuple-element.17) | copy-start | bytes 1179652
  171.8 42.7 %collective-permute-start.2 = (f32[384,256]{1,0:T(8,128)}, f32[384,256]{1,0:T(8,128)S(1)}, u32[]{:S(2)}, u32[]{:S(2)}) collective-permute-start(f32[384,256]{1,0:T(8,128)} %get-tuple-element.20), channel_id=1, source_target_pairs={{0,252},{4,248},{8,244},{12,240},{16,236},{20,232},{24,228},{28,22... | collective-permute-start | bytes 1179656 | tf_op jit(solution)/shard_map/ppermute | solution.py:240
  174.6 37.4 %collective-permute-start.1 = (f32[2,384,1]{2,1,0:T(8,128)}, f32[2,384,1]{2,1,0:T(8,128)S(1)}, u32[]{:S(2)}, u32[]{:S(2)}) collective-permute-start(f32[2,384,1]{2,1,0:T(8,128)} %bitcast.55), channel_id=1, source_target_pairs={{0,252},{4,248},{8,244},{12,240},{16,236},{20,232},{24,228},{28,22... | collective-permute-start | bytes 9224 | tf_op jit(solution)/shard_map/ppermute | solution.py:241
Sparse Core Ops, SparseCore 0:
  10.7 128.4 all-gather.1

commit v6 on v5

--- a/solution.py
+++ b/solution.py
@@ -237,8 +237,12 @@
     a_lo = jnp.where(heavy, place - half, 0)
     o_a, lse_a = self_partial(place, a_lo, place + 1, self_q, kv, tk, (half + 1) // 2 + 1)
     o_a, lse_a, o_b, lse_b = lax.optimization_barrier((o_a, lse_a, o_b, lse_b))
-    o_back = lax.ppermute(o_b, "seq", pairs)
-    lse_back = lax.ppermute(lse_b[:, :, :1], "seq", pairs)
+    heads = lse_b.shape[0]
+    width = o_b.shape[1]
+    packed = jnp.concatenate([o_b, lse_b[:, :, 0].reshape(heads * rows // width, width)], axis=0)
+    packed = lax.ppermute(packed, "seq", pairs)
+    o_back = packed[:rows]
+    lse_back = packed[rows:].reshape(heads, rows, 1)
     la = spread(lse_a[:, :, :1])
     lb = spread(lse_back)
     peak = jnp.maximum(la, lb)

time: 224 us -> 207 us (0.924)
  waiting for transfers between devices: 127 us -> 112 us
    ppermute x2 -> x1, waiting for transfers between devices: 32.8 us -> 18.3 us  [per_device(): packed = lax.ppermute(packed, 'seq', pairs)]
    ppermute x2 -> x1, starting transfers between devices: 5.07 us -> 2.96 us  [per_device(): packed = lax.ppermute(packed, 'seq', pairs)]
  transfers between devices with their start and end apart: 6 -> 5, of which waited for: 4 -> 4; matrix products, arithmetic and copies ran while one was open for 5% -> 5% of each run, Pallas kernels for 5% -> 6%
where the time goes in v6:
time: 207 us
  waiting for transfers between devices  112 us (54%)
  Pallas kernels  38.3 us (19%)
  starting transfers between devices  23.4 us (11%)
  between operations  14.9 us (7%)
  local copies, waits for them, and re-layouts  12.5 us (6%)
  other arithmetic  5 us (2%)
    all_gather x1, waiting for transfers between devices, per_device(): lax.all_gather(jnp.concatenate([self_k, self_v], axis=1), 'seq', axis=0,...  63.5 us
    pallas_call x2, Pallas kernels, self_partial(): pl.pallas_call(self_kernel, grid_spec=grid_spec, out_shape=[jax.ShapeDtyp...  31.8 us
    all_to_all x1, waiting for transfers between devices, per_device(): lax.all_to_all(text_v, 'txt', split_axis=1, concat_axis=0, tiled=True)  22.6 us
    ppermute x1, waiting for transfers between devices, per_device(): packed = lax.ppermute(packed, 'seq', pairs)  18.3 us
    ppermute x1, starting transfers between devices, per_device(): other_q = lax.ppermute(self_q, 'seq', pairs)  11.7 us
    all_to_all x1, waiting for transfers between devices, per_device(): lax.all_to_all(text_k, 'txt', split_axis=1, concat_axis=0, tiled=True)  7.93 us
    pallas_call x1, Pallas kernels, cross_attention(): pl.pallas_call(cross_kernel, grid_spec=grid_spec, out_shape=jax.ShapeDtyp...  6.5 us
    all_to_all x1, starting transfers between devices, per_device(): lax.all_to_all(text_v, 'txt', split_axis=1, concat_axis=0, tiled=True)  4.96 us
  transfers between devices with their start and end apart: 5, of which 4 were waited for; matrix products, arithmetic and copies ran while one was open for 5% of the time, Pallas kernels for 6%

profile of v6, /device:TPU:1, one launch (start us, length us, event | category | flops | bytes accessed | tf_op | source)
XLA Modules:
  0.0 206.5 jit_solution(13942149064566041026)
XLA Ops:
  7.2 0.0 all-gather.2.cloned.1.call-start
  7.2 1.8 pad_maximum_fusion.1
  9.0 0.0 all-gather.2.cloned.1.call-update
  9.1 3.0 %copy.30 = bf16[128,4,8,256]{3,2,0,1:T(8,128)(2,1)} copy(bf16[128,4,8,256]{3,2,1,0:T(8,128)(2,1)} %bitcast.51) | data formatting | bytes 4194304 | tf_op jit(solution)/shard_map/all_to_all | solution.py:218
  12.1 0.0 copy-start
  12.1 5.0 %all-to-all-start.1 = ((bf16[1024,4,256]{2,0,1:T(8,128)(2,1)}), bf16[1024,4,256]{2,0,1:T(8,128)(2,1)}, u32[]{:S(2)}, u32[]{:S(2)}) async-start(bf16[1024,4,256]{2,0,1:T(8,128)(2,1)} %bitcast.49), calls=%async_computation.1 | async-start | bytes 4194304 | tf_op jit(solution)/shard_map/all_to_all | solution.py:218
  17.1 0.0 copy-done
  17.1 1.5 copy.31
  18.5 22.6 %all-to-all-done.1 = bf16[1024,4,256]{2,0,1:T(8,128)(2,1)} async-done(((bf16[1024,4,256]{2,0,1:T(8,128)(2,1)}), bf16[1024,4,256]{2,0,1:T(8,128)(2,1)}, u32[]{:S(2)}, u32[]{:S(2)}) %all-to-all-start.1) | async-done | bytes 2097184 | tf_op jit(solution)/shard_map/all_to_all | solution.py:218
  41.2 0.0 copy-start.4
  41.2 0.0 copy-start.6
  41.2 3.7 %all-to-all-start = ((bf16[1024,4,256]{2,0,1:T(8,128)(2,1)}), bf16[1024,4,256]{2,0,1:T(8,128)(2,1)S(1)}, u32[]{:S(2)}, u32[]{:S(2)}) async-start(bf16[1024,4,256]{2,0,1:T(8,128)(2,1)} %bitcast.50), calls=%async_computation | async-start | bytes 4194304 | tf_op jit(solution)/shard_map/all_to_all | solution.py:217
  44.9 0.0 copy-done.4
  44.9 11.7 %collective-permute-start = (bf16[384,256]{1,0:T(8,128)(2,1)S(1)}, bf16[384,256]{1,0:T(8,128)(2,1)S(1)}, u32[]{:S(2)}, u32[]{:S(2)}) collective-permute-start(bf16[384,256]{1,0:T(8,128)(2,1)S(1)} %copy-done.4), channel_id=1, source_target_pairs={{0,252},{4,248},{8,244},{12,240},{16,236},{20,232},{24,228},{28,22... | collective-permute-start | bytes 589832 | tf_op jit(solution)/shard_map/ppermute | solution.py:233
  56.6 0.0 copy-done.6
  56.6 0.6 reduce_max.9
  58.0 0.7 stack.47.info_ref
  58.7 0.6 stack.42.info_ref
  59.3 0.6 pad_add_fusion.info_ref
  59.9 7.9 %all-to-all-done = bf16[1024,4,256]{2,0,1:T(8,128)(2,1)S(1)} async-done(((bf16[1024,4,256]{2,0,1:T(8,128)(2,1)}), bf16[1024,4,256]{2,0,1:T(8,128)(2,1)S(1)}, u32[]{:S(2)}, u32[]{:S(2)}) %all-to-all-start) | async-done | bytes 2097184 | tf_op jit(solution)/shard_map/all_to_all | solution.py:217
  67.9 0.0 copy-start.1
  67.9 1.3 copy-done.1
  69.2 6.5 %shard_map.86 = bf16[384,256]{1,0:T(8,128)(2,1)} custom-call(s32[4]{0:T(128)} %pad_add_fusion.info_ref, bf16[384,256]{1,0:T(8,128)(2,1)} %q_ref.2, bf16[4096,256]{1,0:T(8,128)(2,1)} %bitcast.53, bf16[4096,256]{1,0:T(8,128)(2,1)} %bitcast.10.v_ref), custom_call_target="tpu_custom_call" | custom-call | flops 1610612736 | bytes 4587520 | tf_op jit(solution)/shard_map/pallas_call | solution.py:199
  75.7 63.5 %all-gather.2.cloned.1.call-done.k_ref.v_ref = bf16[24576,512]{1,0:T(8,128)(2,1)} async-done(((bf16[384,512]{1,0:T(8,128)(2,1)}), bf16[24576,512]{1,0:T(8,128)(2,1)}) %all-gather.2.cloned.1.call-update) | async-done | bytes 25165840 | tf_op jit(solution)/shard_map/all_gather | solution.py:226
  139.2 5.5 %shard_map.87 = (f32[384,256]{1,0:T(8,128)}, f32[2,384,128]{2,1,0:T(8,128)}) custom-call(s32[6]{0:T(128)} %stack.42.info_ref, bf16[384,256]{1,0:T(8,128)(2,1)} %q_ref.3, bf16[24576,512]{1,0:T(8,128)(2,1)} %all-gather.2.cloned.1.call-done.k_ref.v_ref, bf16[24576,512]{1,0:T(8,128)(2,1)} %all-gather.2.cloned.1.call-done.k_ref.v_ref), custom_call_target="tpu_custom_call" | custom-call | flops 2566914048 | bytes 14352384 | tf_op jit(solution)/shard_map/pallas_call | solution.py:126
  144.8 0.0 copy-start.3
  144.8 0.0 collective-permute-done.q_ref
  144.8 0.0 copy-start.5
  144.8 0.7 copy-done.5
  145.5 26.3 %shard_map.88 = (f32[384,256]{1,0:T(8,128)}, f32[2,384,128]{2,1,0:T(8,128)}) custom-call(s32[6]{0:T(128)} %stack.47.info_ref, bf16[384,256]{1,0:T(8,128)(2,1)} %copy-done.5, bf16[24576,512]{1,0:T(8,128)(2,1)} %all-gather.2.cloned.1.call-done.k_ref.v_ref, bf16[24576,512]{1,0:T(8,128)(2,1)} %all-gather.2.cloned.1.call-done.k_ref.v_ref), custom_call_target="tpu_custom_call" | custom-call | flops 2415919104 | bytes 13565952 | tf_op jit(solution)/shard_map/pallas_call | solution.py:126
  171.7 0.0 copy-start.2
  171.7 1.2 slice_reduce_fusion
  173.0 1.0 pad_maximum_fusion
  174.0 3.0 %collective-permute-start.1 = (f32[387,256]{1,0:T(8,128)S(1)}, f32[387,256]{1,0:T(8,128)S(1)}, u32[]{:S(2)}, u32[]{:S(2)}) collective-permute-start(f32[387,256]{1,0:T(8,128)S(1)} %pad_maximum_fusion), channel_id=1, source_target_pairs={{0,252},{4,248},{8,244},{12,240},{16,236},{20,232},{24,228},{28,22... | collective-permute-start | bytes 1188872 | tf_op jit(solution)/shard_map/ppermute | solution.py:243
  177.0 0.0 copy-done.3
  177.0 2.4 %copy.17 = f32[384,2,1]{1,0,2:T(8,128)S(1)} copy(f32[384,2,1]{2,0,1:T(8,128)S(1)} %slice_bitcast_fusion) | data formatting | bytes 6144 | tf_op jit(solution)/shard_map/broadcast_in_dim | solution.py:144
  179.4 18.3 %collective-permute-done.1 = f32[387,256]{1,0:T(8,128)S(1)} collective-permute-done((f32[387,256]{1,0:T(8,128)S(1)}, f32[387,256]{1,0:T(8,128)S(1)}, u32[]{:S(2)}, u32[]{:S(2)}) %collective-permute-start.1) | collective-permute-done | bytes 396320 | tf_op jit(solution)/shard_map/ppermute | solution.py:243
  197.7 0.1 copy.16
  197.8 0.5 broadcast_in_dim.21
  198.3 0.5 broadcast_in_dim.19
  198.8 0.0 copy-done.2
  198.8 0.9 fusion.6
  (4 shorter events, 0.1 us)
Async XLA Ops:
  7.2 132.1 %all-gather.2.cloned.1.call-start = ((), (), s32[]{:S(2)}) async-start(), calls=%async_computation.2 | async-start | bytes 25559040 | tf_op jit(solution)/shard_map/all_gather | solution.py:226
  12.1 5.0 %copy-start = (bf16[1024,1024]{1,0:T(8,128)(2,1)S(1)}, bf16[1024,1024]{1,0:T(8,128)(2,1)}, u32[]{:S(2)}) copy-start(bf16[1024,1024]{1,0:T(8,128)(2,1)} %param.11) | copy-start | bytes 6291460
  12.1 29.1 %all-to-all-start.1 = ((bf16[1024,4,256]{2,0,1:T(8,128)(2,1)}), bf16[1024,4,256]{2,0,1:T(8,128)(2,1)}, u32[]{:S(2)}, u32[]{:S(2)}) async-start(bf16[1024,4,256]{2,0,1:T(8,128)(2,1)} %bitcast.49), calls=%async_computation.1 | async-start | bytes 4194304 | tf_op jit(solution)/shard_map/all_to_all | solution.py:218
  41.2 3.8 %copy-start.4 = (bf16[384,256]{1,0:T(8,128)(2,1)S(1)}, bf16[384,256]{1,0:T(8,128)(2,1)}, u32[]{:S(2)}) copy-start(bf16[384,256]{1,0:T(8,128)(2,1)} %q_ref.3) | copy-start | bytes 589828
  41.2 15.5 %copy-start.6 = (s32[3]{0:T(128)S(1)}, s32[3]{0:T(128)}, u32[]{:S(2)}) copy-start(s32[3]{0:T(128)} %param.13) | copy-start | bytes 40
  41.2 26.7 %all-to-all-start = ((bf16[1024,4,256]{2,0,1:T(8,128)(2,1)}), bf16[1024,4,256]{2,0,1:T(8,128)(2,1)S(1)}, u32[]{:S(2)}, u32[]{:S(2)}) async-start(bf16[1024,4,256]{2,0,1:T(8,128)(2,1)} %bitcast.50), calls=%async_computation | async-start | bytes 4194304 | tf_op jit(solution)/shard_map/all_to_all | solution.py:217
  44.9 99.8 %collective-permute-start = (bf16[384,256]{1,0:T(8,128)(2,1)S(1)}, bf16[384,256]{1,0:T(8,128)(2,1)S(1)}, u32[]{:S(2)}, u32[]{:S(2)}) collective-permute-start(bf16[384,256]{1,0:T(8,128)(2,1)S(1)} %copy-done.4), channel_id=1, source_target_pairs={{0,252},{4,248},{8,244},{12,240},{16,236},{20,232},{24,228},{28,22... | collective-permute-start | bytes 589832 | tf_op jit(solution)/shard_map/ppermute | solution.py:233
  67.9 1.3 copy-start.1
  144.8 32.2 %copy-start.3 = (f32[2,384,128]{2,1,0:T(8,128)S(1)}, f32[2,384,128]{2,1,0:T(8,128)}, u32[]{:S(2)}) copy-start(f32[2,384,128]{2,1,0:T(8,128)} %get-tuple-element.18) | copy-start | bytes 1179652
  144.8 0.7 copy-start.5
  171.7 27.0 %copy-start.2 = (f32[384,256]{1,0:T(8,128)S(1)}, f32[384,256]{1,0:T(8,128)}, u32[]{:S(2)}) copy-start(f32[384,256]{1,0:T(8,128)} %get-tuple-element.17) | copy-start | bytes 1179652
  174.0 23.7 %collective-permute-start.1 = (f32[387,256]{1,0:T(8,128)S(1)}, f32[387,256]{1,0:T(8,128)S(1)}, u32[]{:S(2)}, u32[]{:S(2)}) collective-permute-start(f32[387,256]{1,0:T(8,128)S(1)} %pad_maximum_fusion), channel_id=1, source_target_pairs={{0,252},{4,248},{8,244},{12,240},{16,236},{20,232},{24,228},{28,22... | collective-permute-start | bytes 1188872 | tf_op jit(solution)/shard_map/ppermute | solution.py:243
Sparse Core Ops, SparseCore 0:
  10.7 128.4 all-gather.1

commit v7 on v2

--- a/solution.py
+++ b/solution.py
@@ -16,24 +16,26 @@
 
 NEG_FILL = -1e30
 FACTOR = 1.0 / math.sqrt(HSIZE)
+SCALE2 = FACTOR * 1.4426950408889634
 
 
 def online_step(q, k, v, mask, m_ref, l_ref, acc_ref):
     scores = (
         lax.dot_general(q, k, (((1,), (1,)), ((), ())), preferred_element_type=jnp.float32)
-        * FACTOR
+        * SCALE2
     )
     if mask is not None:
         scores = jnp.where(mask, scores, NEG_FILL)
     m_prev = m_ref[...]
     m_next = jnp.maximum(m_prev, jnp.max(scores, axis=1, keepdims=True))
-    probs = jnp.exp(scores - m_next[:, 0:1])
+    probs = jnp.exp2(scores - m_next[:, 0:1])
     if mask is not None:
         probs = jnp.where(mask, probs, 0.0)
-    alpha = jnp.exp(m_prev - m_next)
-    l_ref[...] = alpha * l_ref[...] + jnp.sum(probs, axis=1, keepdims=True)
-    mixed = jnp.dot(probs.astype(jnp.bfloat16), v, preferred_element_type=jnp.float32)
-    acc_ref[...] = acc_ref[...] * alpha + mixed
+    alpha = jnp.exp2(m_prev - m_next)
+    extended = jnp.concatenate([v, jnp.ones_like(v)], axis=1)
+    mixed = jnp.dot(probs.astype(jnp.bfloat16), extended, preferred_element_type=jnp.float32)
+    l_ref[...] = alpha * l_ref[...] + mixed[:, HSIZE:]
+    acc_ref[...] = acc_ref[...] * alpha + mixed[:, :HSIZE]
     m_ref[...] = m_next
 
 
@@ -181,21 +183,22 @@
 
 def per_device(self_q, self_k, self_v, cross_q, text_k, text_v, lags):
     rows = self_q.shape[0]
-    tk = 2 * rows
     place = lax.axis_index("seq")
 
     whole_keys = lax.all_to_all(text_k, "txt", split_axis=1, concat_axis=0, tiled=True)
     whole_values = lax.all_to_all(text_v, "txt", split_axis=1, concat_axis=0, tiled=True)
-
-    kv = lax.all_gather(jnp.concatenate([self_k, self_v], axis=1), "seq", axis=0, tiled=True)
-    info = jnp.stack([place, (place * rows + rows - 1) // tk]).astype(jnp.int32)
-    self_out = self_attention(info, self_q, kv, tk)
 
     top = jnp.max(lags)
     cross_info = jnp.concatenate(
         [lags.astype(jnp.int32), ((top * TBLK - 1) // 512)[None].astype(jnp.int32)]
     )
     cross_out = cross_attention(cross_info, cross_q, whole_keys, whole_values)
+
+    kv = lax.all_gather(jnp.concatenate([self_k, self_v], axis=1), "seq", axis=0, tiled=True)
+    kv, cross_out = lax.optimization_barrier((kv, cross_out))
+    tk = 4 * rows if kv.shape[0] % (4 * rows) == 0 else rows
+    info = jnp.stack([place, (place * rows + rows - 1) // tk]).astype(jnp.int32)
+    self_out = self_attention(info, self_q, kv, tk)
     return (self_out, cross_out)
 
 

time: 195 us -> 179 us (0.918)
  Pallas kernels: 76.3 us -> 61.3 us
    pallas_call x1, Pallas kernels: 59.6 us -> 42.9 us  [self_attention(): pl.pallas_call(self_kernel, grid_spec=grid_spec, out_shape=jax.ShapeDtype...]
  transfers between devices with their start and end apart: 3 -> 3, of which waited for: 3 -> 3; matrix products, arithmetic and copies ran while one was open for 3% -> 4% of each run, Pallas kernels for 9% -> 10%
where the time goes in v7:
time: 179 us; the launch traced here: 178 us
  waiting for transfers between devices  83.9 us (47%)
  Pallas kernels  61.3 us (34%)
  between operations  14.8 us (8%)
  starting transfers between devices  8.39 us (5%)
  local copies, waits for them, and re-layouts  5.85 us (3%)
  other arithmetic  3.59 us (2%)
    pallas_call x1, Pallas kernels, self_attention(): pl.pallas_call(self_kernel, grid_spec=grid_spec, out_shape=jax.ShapeDtype...  42.9 us
    all_gather x1, waiting for transfers between devices, per_device(): lax.all_gather(jnp.concatenate([self_k, self_v], axis=1), 'seq', axis=0,...  37.2 us
    all_to_all x1, waiting for transfers between devices, per_device(): lax.all_to_all(text_k, 'txt', split_axis=1, concat_axis=0, tiled=True)  24.3 us
    all_to_all x1, waiting for transfers between devices, per_device(): lax.all_to_all(text_v, 'txt', split_axis=1, concat_axis=0, tiled=True)  22.4 us
    pallas_call x1, Pallas kernels, cross_attention(): pl.pallas_call(cross_kernel, grid_spec=grid_spec, out_shape=jax.ShapeDtyp...  18.4 us
    all_to_all x1, starting transfers between devices, per_device(): lax.all_to_all(text_k, 'txt', split_axis=1, concat_axis=0, tiled=True)  4.62 us
    all_to_all x1, starting transfers between devices, per_device(): lax.all_to_all(text_v, 'txt', split_axis=1, concat_axis=0, tiled=True)  3.74 us
  transfers between devices with their start and end apart: 3, of which 3 were waited for; matrix products, arithmetic and copies ran while one was open for 4% of the time, Pallas kernels for 10%

profile of v7, /device:TPU:249, one launch (start us, length us, event | category | flops | bytes accessed | tf_op | source)
XLA Modules:
  0.0 177.7 jit_solution(11964203974998342921)
XLA Ops:
  7.2 0.0 all-gather.2.cloned.1.call-start
  7.2 1.8 %pad_maximum_fusion = bf16[384,512]{1,0:T(8,128)(2,1)} fusion(bf16[384,256]{1,0:T(8,128)(2,1)} %param.9, bf16[384,256]{1,0:T(8,128)(2,1)} %param.8), kind=kLoop, calls=%fused_computation.2 | loop fusion | flops 786432 | bytes 786432 | tf_op jit(solution)/shard_map/concatenate | solution.py:197
  9.0 0.0 all-gather.2.cloned.1.call-update
  9.0 3.1 %copy.16 = bf16[128,4,8,256]{3,2,0,1:T(8,128)(2,1)} copy(bf16[128,4,8,256]{3,2,1,0:T(8,128)(2,1)} %bitcast.17) | data formatting | bytes 4194304 | tf_op jit(solution)/shard_map/all_to_all | solution.py:188
  12.1 0.0 copy-start
  12.1 4.6 %all-to-all-start = ((bf16[1024,4,256]{2,0,1:T(8,128)(2,1)}), bf16[1024,4,256]{2,0,1:T(8,128)(2,1)}, u32[]{:S(2)}, u32[]{:S(2)}) async-start(bf16[1024,4,256]{2,0,1:T(8,128)(2,1)} %bitcast.16), calls=%async_computation | async-start | bytes 4194304 | tf_op jit(solution)/shard_map/all_to_all | solution.py:188
  16.7 0.0 copy-done
  16.7 1.5 copy.15
  18.2 24.3 %all-to-all-done = bf16[1024,4,256]{2,0,1:T(8,128)(2,1)} async-done(((bf16[1024,4,256]{2,0,1:T(8,128)(2,1)}), bf16[1024,4,256]{2,0,1:T(8,128)(2,1)}, u32[]{:S(2)}, u32[]{:S(2)}) %all-to-all-start) | async-done | bytes 2097184 | tf_op jit(solution)/shard_map/all_to_all | solution.py:188
  42.5 0.0 copy-start.2
  42.5 3.7 %all-to-all-start.1 = ((bf16[1024,4,256]{2,0,1:T(8,128)(2,1)}), bf16[1024,4,256]{2,0,1:T(8,128)(2,1)S(1)}, u32[]{:S(2)}, u32[]{:S(2)}) async-start(bf16[1024,4,256]{2,0,1:T(8,128)(2,1)} %bitcast.15), calls=%async_computation.1 | async-start | bytes 4194304 | tf_op jit(solution)/shard_map/all_to_all | solution.py:189
  46.3 0.0 copy-done.2
  46.3 0.6 reduce_max.9
  47.6 0.6 pad_add_fusion.1.info_ref
  48.2 0.6 pad_add_fusion.info_ref
  48.8 22.4 %all-to-all-done.1 = bf16[1024,4,256]{2,0,1:T(8,128)(2,1)S(1)} async-done(((bf16[1024,4,256]{2,0,1:T(8,128)(2,1)}), bf16[1024,4,256]{2,0,1:T(8,128)(2,1)S(1)}, u32[]{:S(2)}, u32[]{:S(2)}) %all-to-all-start.1) | async-done | bytes 2097184 | tf_op jit(solution)/shard_map/all_to_all | solution.py:189
  71.1 0.0 copy-start.1
  71.1 1.3 copy-done.1
  72.5 18.4 %shard_map.86 = bf16[384,256]{1,0:T(8,128)(2,1)} custom-call(s32[4]{0:T(128)} %pad_add_fusion.1.info_ref, bf16[384,256]{1,0:T(8,128)(2,1)} %q_ref.2, bf16[4096,256]{1,0:T(8,128)(2,1)} %bitcast.4.k_ref, bf16[4096,256]{1,0:T(8,128)(2,1)} %bitcast.19), custom_call_target="tpu_custom_call" | custom-call | flops 1610612736 | bytes 4587520 | tf_op jit(solution)/shard_map/pallas_call | solution.py:171
  90.8 37.2 %all-gather.2.cloned.1.call-done.k_ref.v_ref = bf16[24576,512]{1,0:T(8,128)(2,1)} async-done(((bf16[384,512]{1,0:T(8,128)(2,1)}), bf16[24576,512]{1,0:T(8,128)(2,1)}) %all-gather.2.cloned.1.call-update) | async-done | bytes 25165840 | tf_op jit(solution)/shard_map/all_gather | solution.py:197
  128.0 42.9 %shard_map.87 = bf16[384,256]{1,0:T(8,128)(2,1)} custom-call(s32[2]{0:T(128)} %pad_add_fusion.info_ref, bf16[384,256]{1,0:T(8,128)(2,1)} %q_ref.3, bf16[24576,512]{1,0:T(8,128)(2,1)} %all-gather.2.cloned.1.call-done.k_ref.v_ref, bf16[24576,512]{1,0:T(8,128)(2,1)} %all-gather.2.cloned.1.call-done.k_ref.v_ref), custom_call_target="tpu_custom_call" | custom-call | flops 4831838208 | bytes 12976128 | tf_op jit(solution)/shard_map/pallas_call | solution.py:108
Async XLA Ops:
  7.2 120.8 %all-gather.2.cloned.1.call-start = ((), (), s32[]{:S(2)}) async-start(), calls=%async_computation.2 | async-start | bytes 25559040 | tf_op jit(solution)/shard_map/all_gather | solution.py:197
  12.1 4.6 %copy-start = (bf16[1024,1024]{1,0:T(8,128)(2,1)S(1)}, bf16[1024,1024]{1,0:T(8,128)(2,1)}, u32[]{:S(2)}) copy-start(bf16[1024,1024]{1,0:T(8,128)(2,1)} %param.12) | copy-start | bytes 6291460
  12.1 30.4 %all-to-all-start = ((bf16[1024,4,256]{2,0,1:T(8,128)(2,1)}), bf16[1024,4,256]{2,0,1:T(8,128)(2,1)}, u32[]{:S(2)}, u32[]{:S(2)}) async-start(bf16[1024,4,256]{2,0,1:T(8,128)(2,1)} %bitcast.16), calls=%async_computation | async-start | bytes 4194304 | tf_op jit(solution)/shard_map/all_to_all | solution.py:188
  42.5 3.8 %copy-start.2 = (s32[3]{0:T(128)S(1)}, s32[3]{0:T(128)}, u32[]{:S(2)}) copy-start(s32[3]{0:T(128)} %param.13) | copy-start | bytes 40
  42.5 28.6 %all-to-all-start.1 = ((bf16[1024,4,256]{2,0,1:T(8,128)(2,1)}), bf16[1024,4,256]{2,0,1:T(8,128)(2,1)S(1)}, u32[]{:S(2)}, u32[]{:S(2)}) async-start(bf16[1024,4,256]{2,0,1:T(8,128)(2,1)} %bitcast.15), calls=%async_computation.1 | async-start | bytes 4194304 | tf_op jit(solution)/shard_map/all_to_all | solution.py:189
  71.1 1.3 copy-start.1
Sparse Core Ops, SparseCore 0:
  10.7 117.2 all-gather.1

commit v8 on v7

--- a/solution.py
+++ b/solution.py
@@ -196,7 +196,7 @@
 
     kv = lax.all_gather(jnp.concatenate([self_k, self_v], axis=1), "seq", axis=0, tiled=True)
     kv, cross_out = lax.optimization_barrier((kv, cross_out))
-    tk = 4 * rows if kv.shape[0] % (4 * rows) == 0 else rows
+    tk = 8 * rows if kv.shape[0] % (8 * rows) == 0 else rows
     info = jnp.stack([place, (place * rows + rows - 1) // tk]).astype(jnp.int32)
     self_out = self_attention(info, self_q, kv, tk)
     return (self_out, cross_out)

time: 179 us -> 175 us (0.978)
  Pallas kernels: 61.3 us -> 57.5 us
    pallas_call x1, Pallas kernels: 42.9 us -> 39.1 us  [self_attention(): pl.pallas_call(self_kernel, grid_spec=grid_spec, out_shape=jax.ShapeDtype...]
  transfers between devices with their start and end apart: 3 -> 3, of which waited for: 3 -> 3; matrix products, arithmetic and copies ran while one was open for 4% -> 4% of each run, Pallas kernels for 10% -> 11%
where the time goes in v8:
time: 175 us; the launch traced here: 174 us
  waiting for transfers between devices  83.9 us (48%)
  Pallas kernels  57.5 us (33%)
  between operations  14.8 us (8%)
  starting transfers between devices  8.39 us (5%)
  local copies, waits for them, and re-layouts  5.85 us (3%)
  other arithmetic  3.59 us (2%)
    pallas_call x1, Pallas kernels, self_attention(): pl.pallas_call(self_kernel, grid_spec=grid_spec, out_shape=jax.ShapeDtype...  39.1 us
    all_gather x1, waiting for transfers between devices, per_device(): lax.all_gather(jnp.concatenate([self_k, self_v], axis=1), 'seq', axis=0,...  37.2 us
    all_to_all x1, waiting for transfers between devices, per_device(): lax.all_to_all(text_k, 'txt', split_axis=1, concat_axis=0, tiled=True)  24.3 us
    all_to_all x1, waiting for transfers between devices, per_device(): lax.all_to_all(text_v, 'txt', split_axis=1, concat_axis=0, tiled=True)  22.4 us
    pallas_call x1, Pallas kernels, cross_attention(): pl.pallas_call(cross_kernel, grid_spec=grid_spec, out_shape=jax.ShapeDtyp...  18.4 us
    all_to_all x1, starting transfers between devices, per_device(): lax.all_to_all(text_k, 'txt', split_axis=1, concat_axis=0, tiled=True)  4.62 us
    all_to_all x1, starting transfers between devices, per_device(): lax.all_to_all(text_v, 'txt', split_axis=1, concat_axis=0, tiled=True)  3.74 us
  transfers between devices with their start and end apart: 3, of which 3 were waited for; matrix products, arithmetic and copies ran while one was open for 4% of the time, Pallas kernels for 11%

profile of v8, /device:TPU:249, one launch (start us, length us, event | category | flops | bytes accessed | tf_op | source)
XLA Modules:
  0.0 174.0 jit_solution(11318297266535845255)
XLA Ops:
  7.2 0.0 all-gather.2.cloned.1.call-start
  7.2 1.8 %pad_maximum_fusion = bf16[384,512]{1,0:T(8,128)(2,1)} fusion(bf16[384,256]{1,0:T(8,128)(2,1)} %param.9, bf16[384,256]{1,0:T(8,128)(2,1)} %param.8), kind=kLoop, calls=%fused_computation.2 | loop fusion | flops 786432 | bytes 786432 | tf_op jit(solution)/shard_map/concatenate | solution.py:197
  9.0 0.0 all-gather.2.cloned.1.call-update
  9.0 3.1 %copy.16 = bf16[128,4,8,256]{3,2,0,1:T(8,128)(2,1)} copy(bf16[128,4,8,256]{3,2,1,0:T(8,128)(2,1)} %bitcast.17) | data formatting | bytes 4194304 | tf_op jit(solution)/shard_map/all_to_all | solution.py:188
  12.1 0.0 copy-start
  12.1 4.6 %all-to-all-start = ((bf16[1024,4,256]{2,0,1:T(8,128)(2,1)}), bf16[1024,4,256]{2,0,1:T(8,128)(2,1)}, u32[]{:S(2)}, u32[]{:S(2)}) async-start(bf16[1024,4,256]{2,0,1:T(8,128)(2,1)} %bitcast.16), calls=%async_computation | async-start | bytes 4194304 | tf_op jit(solution)/shard_map/all_to_all | solution.py:188
  16.7 0.0 copy-done
  16.7 1.5 copy.15
  18.2 24.3 %all-to-all-done = bf16[1024,4,256]{2,0,1:T(8,128)(2,1)} async-done(((bf16[1024,4,256]{2,0,1:T(8,128)(2,1)}), bf16[1024,4,256]{2,0,1:T(8,128)(2,1)}, u32[]{:S(2)}, u32[]{:S(2)}) %all-to-all-start) | async-done | bytes 2097184 | tf_op jit(solution)/shard_map/all_to_all | solution.py:188
  42.5 0.0 copy-start.2
  42.5 3.7 %all-to-all-start.1 = ((bf16[1024,4,256]{2,0,1:T(8,128)(2,1)}), bf16[1024,4,256]{2,0,1:T(8,128)(2,1)S(1)}, u32[]{:S(2)}, u32[]{:S(2)}) async-start(bf16[1024,4,256]{2,0,1:T(8,128)(2,1)} %bitcast.15), calls=%async_computation.1 | async-start | bytes 4194304 | tf_op jit(solution)/shard_map/all_to_all | solution.py:189
  46.3 0.0 copy-done.2
  46.3 0.6 reduce_max.9
  47.6 0.6 pad_add_fusion.1.info_ref
  48.2 0.6 pad_add_fusion.info_ref
  48.8 22.4 %all-to-all-done.1 = bf16[1024,4,256]{2,0,1:T(8,128)(2,1)S(1)} async-done(((bf16[1024,4,256]{2,0,1:T(8,128)(2,1)}), bf16[1024,4,256]{2,0,1:T(8,128)(2,1)S(1)}, u32[]{:S(2)}, u32[]{:S(2)}) %all-to-all-start.1) | async-done | bytes 2097184 | tf_op jit(solution)/shard_map/all_to_all | solution.py:189
  71.1 0.0 copy-start.1
  71.1 1.3 copy-done.1
  72.5 18.4 %shard_map.86 = bf16[384,256]{1,0:T(8,128)(2,1)} custom-call(s32[4]{0:T(128)} %pad_add_fusion.1.info_ref, bf16[384,256]{1,0:T(8,128)(2,1)} %q_ref.2, bf16[4096,256]{1,0:T(8,128)(2,1)} %bitcast.4.k_ref, bf16[4096,256]{1,0:T(8,128)(2,1)} %bitcast.19), custom_call_target="tpu_custom_call" | custom-call | flops 1610612736 | bytes 4587520 | tf_op jit(solution)/shard_map/pallas_call | solution.py:171
  90.8 37.2 %all-gather.2.cloned.1.call-done.k_ref.v_ref = bf16[24576,512]{1,0:T(8,128)(2,1)} async-done(((bf16[384,512]{1,0:T(8,128)(2,1)}), bf16[24576,512]{1,0:T(8,128)(2,1)}) %all-gather.2.cloned.1.call-update) | async-done | bytes 25165840 | tf_op jit(solution)/shard_map/all_gather | solution.py:197
  128.0 39.1 %shard_map.87 = bf16[384,256]{1,0:T(8,128)(2,1)} custom-call(s32[2]{0:T(128)} %pad_add_fusion.info_ref, bf16[384,256]{1,0:T(8,128)(2,1)} %q_ref.3, bf16[24576,512]{1,0:T(8,128)(2,1)} %all-gather.2.cloned.1.call-done.k_ref.v_ref, bf16[24576,512]{1,0:T(8,128)(2,1)} %all-gather.2.cloned.1.call-done.k_ref.v_ref), custom_call_target="tpu_custom_call" | custom-call | flops 4831838208 | bytes 12976128 | tf_op jit(solution)/shard_map/pallas_call | solution.py:108
Async XLA Ops:
  7.2 120.8 %all-gather.2.cloned.1.call-start = ((), (), s32[]{:S(2)}) async-start(), calls=%async_computation.2 | async-start | bytes 25559040 | tf_op jit(solution)/shard_map/all_gather | solution.py:197
  12.1 4.6 %copy-start = (bf16[1024,1024]{1,0:T(8,128)(2,1)S(1)}, bf16[1024,1024]{1,0:T(8,128)(2,1)}, u32[]{:S(2)}) copy-start(bf16[1024,1024]{1,0:T(8,128)(2,1)} %param.12) | copy-start | bytes 6291460
  12.1 30.4 %all-to-all-start = ((bf16[1024,4,256]{2,0,1:T(8,128)(2,1)}), bf16[1024,4,256]{2,0,1:T(8,128)(2,1)}, u32[]{:S(2)}, u32[]{:S(2)}) async-start(bf16[1024,4,256]{2,0,1:T(8,128)(2,1)} %bitcast.16), calls=%async_computation | async-start | bytes 4194304 | tf_op jit(solution)/shard_map/all_to_all | solution.py:188
  42.5 3.8 %copy-start.2 = (s32[3]{0:T(128)S(1)}, s32[3]{0:T(128)}, u32[]{:S(2)}) copy-start(s32[3]{0:T(128)} %param.13) | copy-start | bytes 40
  42.5 28.6 %all-to-all-start.1 = ((bf16[1024,4,256]{2,0,1:T(8,128)(2,1)}), bf16[1024,4,256]{2,0,1:T(8,128)(2,1)S(1)}, u32[]{:S(2)}, u32[]{:S(2)}) async-start(bf16[1024,4,256]{2,0,1:T(8,128)(2,1)} %bitcast.15), calls=%async_computation.1 | async-start | bytes 4194304 | tf_op jit(solution)/shard_map/all_to_all | solution.py:189
  71.1 1.3 copy-start.1
Sparse Core Ops, SparseCore 0:
  10.7 117.2 all-gather.1

commit v9 on v8

--- a/solution.py
+++ b/solution.py
@@ -196,7 +196,7 @@
 
     kv = lax.all_gather(jnp.concatenate([self_k, self_v], axis=1), "seq", axis=0, tiled=True)
     kv, cross_out = lax.optimization_barrier((kv, cross_out))
-    tk = 8 * rows if kv.shape[0] % (8 * rows) == 0 else rows
+    tk = 16 * rows if kv.shape[0] % (16 * rows) == 0 else rows
     info = jnp.stack([place, (place * rows + rows - 1) // tk]).astype(jnp.int32)
     self_out = self_attention(info, self_q, kv, tk)
     return (self_out, cross_out)

time: 175 us -> 179 us (1.023)
  the two profiles are of different devices: /device:TPU:249 before, /device:TPU:25 now
where the time goes in v9:
time: 179 us; the launch traced here: 178 us
  waiting for transfers between devices  89.4 us (50%)
  Pallas kernels  56.4 us (32%)
  between operations  14.8 us (8%)
  starting transfers between devices  8.4 us (5%)
  local copies, waits for them, and re-layouts  5.85 us (3%)
  other arithmetic  3.59 us (2%)
    all_gather x1, waiting for transfers between devices, per_device(): lax.all_gather(jnp.concatenate([self_k, self_v], axis=1), 'seq', axis=0,...  42.7 us
    pallas_call x1, Pallas kernels, self_attention(): pl.pallas_call(self_kernel, grid_spec=grid_spec, out_shape=jax.ShapeDtype...  39.1 us
    all_to_all x1, waiting for transfers between devices, per_device(): lax.all_to_all(text_k, 'txt', split_axis=1, concat_axis=0, tiled=True)  24.3 us
    all_to_all x1, waiting for transfers between devices, per_device(): lax.all_to_all(text_v, 'txt', split_axis=1, concat_axis=0, tiled=True)  22.4 us
    pallas_call x1, Pallas kernels, cross_attention(): pl.pallas_call(cross_kernel, grid_spec=grid_spec, out_shape=jax.ShapeDtyp...  17.3 us
    all_to_all x1, starting transfers between devices, per_device(): lax.all_to_all(text_k, 'txt', split_axis=1, concat_axis=0, tiled=True)  4.62 us
    all_to_all x1, starting transfers between devices, per_device(): lax.all_to_all(text_v, 'txt', split_axis=1, concat_axis=0, tiled=True)  3.75 us
  transfers between devices with their start and end apart: 3, of which 3 were waited for; matrix products, arithmetic and copies ran while one was open for 4% of the time, Pallas kernels for 10%

profile of v9, /device:TPU:25, one launch (start us, length us, event | category | flops | bytes accessed | tf_op | source)
XLA Modules:
  0.0 178.4 jit_solution(14299281808372764289)
XLA Ops:
  7.2 0.0 all-gather.2.cloned.1.call-start
  7.2 1.8 %pad_maximum_fusion = bf16[384,512]{1,0:T(8,128)(2,1)} fusion(bf16[384,256]{1,0:T(8,128)(2,1)} %param.9, bf16[384,256]{1,0:T(8,128)(2,1)} %param.8), kind=kLoop, calls=%fused_computation.2 | loop fusion | flops 786432 | bytes 786432 | tf_op jit(solution)/shard_map/concatenate | solution.py:197
  9.0 0.0 all-gather.2.cloned.1.call-update
  9.0 3.1 %copy.16 = bf16[128,4,8,256]{3,2,0,1:T(8,128)(2,1)} copy(bf16[128,4,8,256]{3,2,1,0:T(8,128)(2,1)} %bitcast.17) | data formatting | bytes 4194304 | tf_op jit(solution)/shard_map/all_to_all | solution.py:188
  12.1 0.0 copy-start
  12.1 4.6 %all-to-all-start = ((bf16[1024,4,256]{2,0,1:T(8,128)(2,1)}), bf16[1024,4,256]{2,0,1:T(8,128)(2,1)}, u32[]{:S(2)}, u32[]{:S(2)}) async-start(bf16[1024,4,256]{2,0,1:T(8,128)(2,1)} %bitcast.16), calls=%async_computation | async-start | bytes 4194304 | tf_op jit(solution)/shard_map/all_to_all | solution.py:188
  16.7 0.0 copy-done
  16.7 1.5 copy.15
  18.2 24.3 %all-to-all-done = bf16[1024,4,256]{2,0,1:T(8,128)(2,1)} async-done(((bf16[1024,4,256]{2,0,1:T(8,128)(2,1)}), bf16[1024,4,256]{2,0,1:T(8,128)(2,1)}, u32[]{:S(2)}, u32[]{:S(2)}) %all-to-all-start) | async-done | bytes 2097184 | tf_op jit(solution)/shard_map/all_to_all | solution.py:188
  42.5 0.0 copy-start.2
  42.5 3.7 %all-to-all-start.1 = ((bf16[1024,4,256]{2,0,1:T(8,128)(2,1)}), bf16[1024,4,256]{2,0,1:T(8,128)(2,1)S(1)}, u32[]{:S(2)}, u32[]{:S(2)}) async-start(bf16[1024,4,256]{2,0,1:T(8,128)(2,1)} %bitcast.15), calls=%async_computation.1 | async-start | bytes 4194304 | tf_op jit(solution)/shard_map/all_to_all | solution.py:189
  46.3 0.0 copy-done.2
  46.3 0.6 reduce_max.9
  47.6 0.6 pad_add_fusion.1.info_ref
  48.2 0.6 pad_add_fusion.info_ref
  48.8 22.4 %all-to-all-done.1 = bf16[1024,4,256]{2,0,1:T(8,128)(2,1)S(1)} async-done(((bf16[1024,4,256]{2,0,1:T(8,128)(2,1)}), bf16[1024,4,256]{2,0,1:T(8,128)(2,1)S(1)}, u32[]{:S(2)}, u32[]{:S(2)}) %all-to-all-start.1) | async-done | bytes 2097184 | tf_op jit(solution)/shard_map/all_to_all | solution.py:189
  71.2 0.0 copy-start.1
  71.2 1.3 copy-done.1
  72.5 17.3 %shard_map.86 = bf16[384,256]{1,0:T(8,128)(2,1)} custom-call(s32[4]{0:T(128)} %pad_add_fusion.1.info_ref, bf16[384,256]{1,0:T(8,128)(2,1)} %q_ref.2, bf16[4096,256]{1,0:T(8,128)(2,1)} %bitcast.4.k_ref, bf16[4096,256]{1,0:T(8,128)(2,1)} %bitcast.19), custom_call_target="tpu_custom_call" | custom-call | flops 1610612736 | bytes 4587520 | tf_op jit(solution)/shard_map/pallas_call | solution.py:171
  89.8 42.7 %all-gather.2.cloned.1.call-done.k_ref.v_ref = bf16[24576,512]{1,0:T(8,128)(2,1)} async-done(((bf16[384,512]{1,0:T(8,128)(2,1)}), bf16[24576,512]{1,0:T(8,128)(2,1)}) %all-gather.2.cloned.1.call-update) | async-done | bytes 25165840 | tf_op jit(solution)/shard_map/all_gather | solution.py:197
  132.5 39.1 %shard_map.87 = bf16[384,256]{1,0:T(8,128)(2,1)} custom-call(s32[2]{0:T(128)} %pad_add_fusion.info_ref, bf16[384,256]{1,0:T(8,128)(2,1)} %q_ref.3, bf16[24576,512]{1,0:T(8,128)(2,1)} %all-gather.2.cloned.1.call-done.k_ref.v_ref, bf16[24576,512]{1,0:T(8,128)(2,1)} %all-gather.2.cloned.1.call-done.k_ref.v_ref), custom_call_target="tpu_custom_call" | custom-call | flops 4831838208 | bytes 12976128 | tf_op jit(solution)/shard_map/pallas_call | solution.py:108
Async XLA Ops:
  7.2 125.3 %all-gather.2.cloned.1.call-start = ((), (), s32[]{:S(2)}) async-start(), calls=%async_computation.2 | async-start | bytes 25559040 | tf_op jit(solution)/shard_map/all_gather | solution.py:197
  12.1 4.6 %copy-start = (bf16[1024,1024]{1,0:T(8,128)(2,1)S(1)}, bf16[1024,1024]{1,0:T(8,128)(2,1)}, u32[]{:S(2)}) copy-start(bf16[1024,1024]{1,0:T(8,128)(2,1)} %param.12) | copy-start | bytes 6291460
  12.1 30.4 %all-to-all-start = ((bf16[1024,4,256]{2,0,1:T(8,128)(2,1)}), bf16[1024,4,256]{2,0,1:T(8,128)(2,1)}, u32[]{:S(2)}, u32[]{:S(2)}) async-start(bf16[1024,4,256]{2,0,1:T(8,128)(2,1)} %bitcast.16), calls=%async_computation | async-start | bytes 4194304 | tf_op jit(solution)/shard_map/all_to_all | solution.py:188
  42.5 3.8 %copy-start.2 = (s32[3]{0:T(128)S(1)}, s32[3]{0:T(128)}, u32[]{:S(2)}) copy-start(s32[3]{0:T(128)} %param.13) | copy-start | bytes 40
  42.5 28.6 %all-to-all-start.1 = ((bf16[1024,4,256]{2,0,1:T(8,128)(2,1)}), bf16[1024,4,256]{2,0,1:T(8,128)(2,1)S(1)}, u32[]{:S(2)}, u32[]{:S(2)}) async-start(bf16[1024,4,256]{2,0,1:T(8,128)(2,1)} %bitcast.15), calls=%async_computation.1 | async-start | bytes 4194304 | tf_op jit(solution)/shard_map/all_to_all | solution.py:189
  71.2 1.3 copy-start.1
Sparse Core Ops, SparseCore 0:
  10.7 121.7 all-gather.1

commit v10 on v8

--- a/solution.py
+++ b/solution.py
@@ -66,11 +66,29 @@
     def _():
         run(None)
 
-    @pl.when(kb == last)
-    def _():
-        r = lax.broadcasted_iota(jnp.int32, (rows, tk), 0) + place * rows
-        j = lax.broadcasted_iota(jnp.int32, (rows, tk), 1) + kb * tk
-        run(j <= r)
+    diag = place - kb * (tk // rows)
+    for piece in range(tk // rows):
+        keys = slice(piece * rows, (piece + 1) * rows)
+
+        @pl.when(jnp.logical_and(kb == last, piece < diag))
+        def _():
+            for h in range(heads):
+                cols = slice(h * HSIZE, (h + 1) * HSIZE)
+                online_step(
+                    q_ref[:, cols], k_ref[keys, cols], v_ref[keys, cols], None,
+                    m_ref.at[h], l_ref.at[h], acc_ref.at[h],
+                )
+
+        @pl.when(jnp.logical_and(kb == last, piece == diag))
+        def _():
+            r = lax.broadcasted_iota(jnp.int32, (rows, rows), 0)
+            j = lax.broadcasted_iota(jnp.int32, (rows, rows), 1)
+            for h in range(heads):
+                cols = slice(h * HSIZE, (h + 1) * HSIZE)
+                online_step(
+                    q_ref[:, cols], k_ref[keys, cols], v_ref[keys, cols], j <= r,
+                    m_ref.at[h], l_ref.at[h], acc_ref.at[h],
+                )
 
     @pl.when(kb == nkb - 1)
     def _():

time: 175 us -> 177 us (1.011)
  Pallas kernels: 57.5 us -> 60.1 us
    pallas_call x1, Pallas kernels: 39.1 us -> 41.7 us  [self_attention(): pl.pallas_call(self_kernel, grid_spec=grid_spec, out_shape=jax.ShapeDtype...]
  transfers between devices with their start and end apart: 3 -> 3, of which waited for: 3 -> 3; matrix products, arithmetic and copies ran while one was open for 4% -> 4% of each run, Pallas kernels for 11% -> 10%
where the time goes in v10:
time: 177 us
  waiting for transfers between devices  83.9 us (47%)
  Pallas kernels  60.1 us (34%)
  between operations  14.8 us (8%)
  starting transfers between devices  8.39 us (5%)
  local copies, waits for them, and re-layouts  5.85 us (3%)
  other arithmetic  3.59 us (2%)
    pallas_call x1, Pallas kernels, self_attention(): pl.pallas_call(self_kernel, grid_spec=grid_spec, out_shape=jax.ShapeDtype...  41.7 us
    all_gather x1, waiting for transfers between devices, per_device(): lax.all_gather(jnp.concatenate([self_k, self_v], axis=1), 'seq', axis=0,...  37.2 us
    all_to_all x1, waiting for transfers between devices, per_device(): lax.all_to_all(text_k, 'txt', split_axis=1, concat_axis=0, tiled=True)  24.3 us
    all_to_all x1, waiting for transfers between devices, per_device(): lax.all_to_all(text_v, 'txt', split_axis=1, concat_axis=0, tiled=True)  22.4 us
    pallas_call x1, Pallas kernels, cross_attention(): pl.pallas_call(cross_kernel, grid_spec=grid_spec, out_shape=jax.ShapeDtyp...  18.4 us
    all_to_all x1, starting transfers between devices, per_device(): lax.all_to_all(text_k, 'txt', split_axis=1, concat_axis=0, tiled=True)  4.62 us
    all_to_all x1, starting transfers between devices, per_device(): lax.all_to_all(text_v, 'txt', split_axis=1, concat_axis=0, tiled=True)  3.74 us
  transfers between devices with their start and end apart: 3, of which 3 were waited for; matrix products, arithmetic and copies ran while one was open for 4% of the time, Pallas kernels for 10%

profile of v10, /device:TPU:249, one launch (start us, length us, event | category | flops | bytes accessed | tf_op | source)
XLA Modules:
  0.0 176.5 jit_solution(9549129561180099291)
XLA Ops:
  7.2 0.0 all-gather.2.cloned.1.call-start
  7.2 1.8 %pad_maximum_fusion = bf16[384,512]{1,0:T(8,128)(2,1)} fusion(bf16[384,256]{1,0:T(8,128)(2,1)} %param.9, bf16[384,256]{1,0:T(8,128)(2,1)} %param.8), kind=kLoop, calls=%fused_computation.2 | loop fusion | flops 786432 | bytes 786432 | tf_op jit(solution)/shard_map/concatenate | solution.py:215
  9.0 0.0 all-gather.2.cloned.1.call-update
  9.0 3.1 %copy.16 = bf16[128,4,8,256]{3,2,0,1:T(8,128)(2,1)} copy(bf16[128,4,8,256]{3,2,1,0:T(8,128)(2,1)} %bitcast.17) | data formatting | bytes 4194304 | tf_op jit(solution)/shard_map/all_to_all | solution.py:206
  12.1 0.0 copy-start
  12.1 4.6 %all-to-all-start = ((bf16[1024,4,256]{2,0,1:T(8,128)(2,1)}), bf16[1024,4,256]{2,0,1:T(8,128)(2,1)}, u32[]{:S(2)}, u32[]{:S(2)}) async-start(bf16[1024,4,256]{2,0,1:T(8,128)(2,1)} %bitcast.16), calls=%async_computation | async-start | bytes 4194304 | tf_op jit(solution)/shard_map/all_to_all | solution.py:206
  16.7 0.0 copy-done
  16.7 1.5 copy.15
  18.2 24.3 %all-to-all-done = bf16[1024,4,256]{2,0,1:T(8,128)(2,1)} async-done(((bf16[1024,4,256]{2,0,1:T(8,128)(2,1)}), bf16[1024,4,256]{2,0,1:T(8,128)(2,1)}, u32[]{:S(2)}, u32[]{:S(2)}) %all-to-all-start) | async-done | bytes 2097184 | tf_op jit(solution)/shard_map/all_to_all | solution.py:206
  42.5 0.0 copy-start.2
  42.5 3.7 %all-to-all-start.1 = ((bf16[1024,4,256]{2,0,1:T(8,128)(2,1)}), bf16[1024,4,256]{2,0,1:T(8,128)(2,1)S(1)}, u32[]{:S(2)}, u32[]{:S(2)}) async-start(bf16[1024,4,256]{2,0,1:T(8,128)(2,1)} %bitcast.15), calls=%async_computation.1 | async-start | bytes 4194304 | tf_op jit(solution)/shard_map/all_to_all | solution.py:207
  46.3 0.0 copy-done.2
  46.3 0.6 reduce_max.9
  47.6 0.6 pad_add_fusion.1.info_ref
  48.2 0.6 pad_add_fusion.info_ref
  48.8 22.4 %all-to-all-done.1 = bf16[1024,4,256]{2,0,1:T(8,128)(2,1)S(1)} async-done(((bf16[1024,4,256]{2,0,1:T(8,128)(2,1)}), bf16[1024,4,256]{2,0,1:T(8,128)(2,1)S(1)}, u32[]{:S(2)}, u32[]{:S(2)}) %all-to-all-start.1) | async-done | bytes 2097184 | tf_op jit(solution)/shard_map/all_to_all | solution.py:207
  71.1 0.0 copy-start.1
  71.1 1.3 copy-done.1
  72.5 18.4 %shard_map.86 = bf16[384,256]{1,0:T(8,128)(2,1)} custom-call(s32[4]{0:T(128)} %pad_add_fusion.1.info_ref, bf16[384,256]{1,0:T(8,128)(2,1)} %q_ref.2, bf16[4096,256]{1,0:T(8,128)(2,1)} %bitcast.4.k_ref, bf16[4096,256]{1,0:T(8,128)(2,1)} %bitcast.19), custom_call_target="tpu_custom_call" | custom-call | flops 1610612736 | bytes 4587520 | tf_op jit(solution)/shard_map/pallas_call | solution.py:189
  90.8 37.2 %all-gather.2.cloned.1.call-done.k_ref.v_ref = bf16[24576,512]{1,0:T(8,128)(2,1)} async-done(((bf16[384,512]{1,0:T(8,128)(2,1)}), bf16[24576,512]{1,0:T(8,128)(2,1)}) %all-gather.2.cloned.1.call-update) | async-done | bytes 25165840 | tf_op jit(solution)/shard_map/all_gather | solution.py:215
  128.0 41.7 %shard_map.87 = bf16[384,256]{1,0:T(8,128)(2,1)} custom-call(s32[2]{0:T(128)} %pad_add_fusion.info_ref, bf16[384,256]{1,0:T(8,128)(2,1)} %q_ref.3, bf16[24576,512]{1,0:T(8,128)(2,1)} %all-gather.2.cloned.1.call-done.k_ref.v_ref, bf16[24576,512]{1,0:T(8,128)(2,1)} %all-gather.2.cloned.1.call-done.k_ref.v_ref), custom_call_target="tpu_custom_call" | custom-call | flops 4831838208 | bytes 12976128 | tf_op jit(solution)/shard_map/pallas_call | solution.py:126
Async XLA Ops:
  7.2 120.8 %all-gather.2.cloned.1.call-start = ((), (), s32[]{:S(2)}) async-start(), calls=%async_computation.2 | async-start | bytes 25559040 | tf_op jit(solution)/shard_map/all_gather | solution.py:215
  12.1 4.6 %copy-start = (bf16[1024,1024]{1,0:T(8,128)(2,1)S(1)}, bf16[1024,1024]{1,0:T(8,128)(2,1)}, u32[]{:S(2)}) copy-start(bf16[1024,1024]{1,0:T(8,128)(2,1)} %param.12) | copy-start | bytes 6291460
  12.1 30.4 %all-to-all-start = ((bf16[1024,4,256]{2,0,1:T(8,128)(2,1)}), bf16[1024,4,256]{2,0,1:T(8,128)(2,1)}, u32[]{:S(2)}, u32[]{:S(2)}) async-start(bf16[1024,4,256]{2,0,1:T(8,128)(2,1)} %bitcast.16), calls=%async_computation | async-start | bytes 4194304 | tf_op jit(solution)/shard_map/all_to_all | solution.py:206
  42.5 3.8 %copy-start.2 = (s32[3]{0:T(128)S(1)}, s32[3]{0:T(128)}, u32[]{:S(2)}) copy-start(s32[3]{0:T(128)} %param.13) | copy-start | bytes 40
  42.5 28.6 %all-to-all-start.1 = ((bf16[1024,4,256]{2,0,1:T(8,128)(2,1)}), bf16[1024,4,256]{2,0,1:T(8,128)(2,1)S(1)}, u32[]{:S(2)}, u32[]{:S(2)}) async-start(bf16[1024,4,256]{2,0,1:T(8,128)(2,1)} %bitcast.15), calls=%async_computation.1 | async-start | bytes 4194304 | tf_op jit(solution)/shard_map/all_to_all | solution.py:207
  71.1 1.3 copy-start.1
Sparse Core Ops, SparseCore 0:
  10.7 117.2 all-gather.1
